TPU v7x, 256 devices: a whole 4x4x8 slice. The times are simulated.
256 devices in a mesh: space: 64 (over x_hi, y, z), dp: 4 (over x_lo, core).
Axes of the slice: x: 4 (x_hi: 2, x_lo: 2; x = x_hi * 2 + x_lo), y: 4, z: 8, core: 2. Of those that a mesh axis runs over, the one named last changes fastest.
Arguments:
- input_states: bfloat16 [4, 64, 200, 1024], P('dp', 'space'), may hold values from -6 to 6
- loss_sensitivity: bfloat16 [4, 64, 200, 1024], P('dp', 'space'), may hold values from -6 to 6
- ocean: int32 [64, 1024], P('space'), may hold values 0 or 1
- neighbours: int32 [64, 8], P('space'), may hold values from -1 to 63, as said below
- fold_flag: int32 [64], P('space'), may hold values from 0 to 1, as said below
- w_first: bfloat16 [9, 200, 200], replicated, may hold values from -0.125 to 0.125
- w_second: bfloat16 [9, 200, 200], replicated, may hold values from -0.125 to 0.125
Outputs:
- prediction: bfloat16 [4, 64, 200, 1024], P('dp', 'space')
- earlier_kernel_slope: float32 [9, 200, 200], replicated
- latter_kernel_slope: float32 [9, 200, 200], replicated
Inputs may be any that keep to these rules, and one draw needn't show every extreme that they name: Tiles sit on a grid of 6 x 16 tile positions, some of them land; the ocean tiles carry numbers 0 to 63 in no particular order of positions; longitude wraps; the top row's northern neighbour is the mirrored tile of the same row (fold_flag 1) and its diagonal northern neighbours are -1. The relation is symmetric: if u is t's neighbour in one direction, t is u's in the opposite one (north for north across the fold). `fold_flag`: 1 exactly for tiles of the top tile row.
All inputs are finite; a program needn't handle non-finite values. No bound on the sum of `ocean` on one device may be relied on, other than what follows from the above.
Results may differ from a plain program's by a relative error of at most 0.005.
Values may be sent and summed in bfloat16 or wider, within the bound.
No kernel may reach another device: no remote copies, remote signals or barrier semaphores. Data moves between devices by JAX's collectives and lax.ppermute only.
A program may use at most 64 MiB of HBM per device.

v0:
```python
import jax
import jax.numpy as jnp
from jax import lax
from jax.sharding import PartitionSpec as P

SIDE = 32


SQRT_TWO_PI = 0.7978845608028654
CUBIC = 0.044715


def gelu_pair(a):
    inner = SQRT_TWO_PI * (a + CUBIC * a * a * a)
    tangent = jnp.tanh(inner)
    value = 0.5 * a * (1.0 + tangent)
    slope = 0.5 * (1.0 + tangent) + 0.5 * a * (1.0 - tangent * tangent) * SQRT_TWO_PI * (
        1.0 + 3.0 * CUBIC * a * a
    )
    return (value, slope)


def edge_strips(field):
    patch_extent = field.shape[2]
    return jnp.concatenate(
        [
            field[:, :, 0, :],
            field[:, :, patch_extent - 1, :],
            field[:, :, :, 0],
            field[:, :, :, patch_extent - 1],
        ],
        axis=2,
    )


def strip_parts(piece, neighbours, fold_flag):
    amount = piece.shape[0]
    patch_extent = piece.shape[2] // 4

    def pick(k):
        index = neighbours[:, k]
        valid = ((index >= 0) & (index < amount)).astype(piece.dtype)
        return jnp.take(piece, jnp.clip(index, 0, amount - 1), axis=0) * valid[:, None, None]

    from_north = pick(0)
    north = jnp.where(
        (fold_flag == 1)[:, None, None],
        from_north[:, :, patch_extent : 2 * patch_extent][:, :, ::-1],
        from_north[:, :, 0:patch_extent],
    )
    south = pick(1)[:, :, patch_extent : 2 * patch_extent]
    east = pick(2)[:, :, 2 * patch_extent : 3 * patch_extent]
    west = pick(3)[:, :, 3 * patch_extent : 4 * patch_extent]
    corners = jnp.stack(
        [
            pick(4)[:, :, 0],
            pick(5)[:, :, patch_extent - 1],
            pick(6)[:, :, patch_extent],
            pick(7)[:, :, 2 * patch_extent - 1],
        ],
        axis=-1,
    )
    return (north, south, east, west, corners)


def collect_rims(strips, neighbours, fold_flag):
    found = strip_parts(lax.all_gather(strips, "space", axis=0, tiled=True), neighbours, fold_flag)
    return tuple((b for b in found))


def padded_tiles(field, parts):
    north, south, east, west, corners = parts
    middle = jnp.concatenate([west[..., None], field, east[..., None]], axis=3)
    bottom = jnp.concatenate([corners[:, :, 3:4], south, corners[:, :, 2:3]], axis=2)[:, :, None, :]
    top = jnp.concatenate([corners[:, :, 1:2], north, corners[:, :, 0:1]], axis=2)[:, :, None, :]
    return jnp.concatenate([bottom, middle, top], axis=2)


def window(padded, shift_r, shift_c):
    patch_extent = padded.shape[2] - 2
    part = padded[
        :, :, 1 + shift_r : 1 + shift_r + patch_extent, 1 + shift_c : 1 + shift_c + patch_extent
    ]
    return part.reshape(padded.shape[0], padded.shape[1], patch_extent * patch_extent)


def conv_forward(padded, weights):
    total = None
    for k in range(9):
        term = jnp.einsum(
            "oi,tic->toc",
            weights[k],
            window(padded, k // 3 - 1, k % 3 - 1),
            preferred_element_type=jnp.float32,
        )
        total = term if total is None else total + term
    return total


def conv_adjoint(padded, weights):
    total = None
    for k in range(9):
        term = jnp.einsum(
            "oi,toc->tic",
            weights[k],
            window(padded, 1 - k // 3, 1 - k % 3),
            preferred_element_type=jnp.float32,
        )
        total = term if total is None else total + term
    return total


def weight_grad(grads, padded):
    return jnp.stack(
        [
            jnp.einsum(
                "toc,tic->oi",
                grads,
                window(padded, k // 3 - 1, k % 3 - 1),
                preferred_element_type=jnp.float32,
            )
            for k in range(9)
        ],
        axis=0,
    )


def body(input_states, loss_sensitivity, ocean, neighbours, fold_flag, w_first, w_second):
    tiles = input_states[0]
    patch_total, feature_depth, cells = tiles.shape
    patch_extent = SIDE
    inputs = tiles.reshape(patch_total, feature_depth, patch_extent, patch_extent)
    water_indicator = ocean.astype(jnp.float32)[:, None, :]
    masked_grad = (loss_sensitivity[0].astype(jnp.float32) * water_indicator).astype(jnp.bfloat16)
    grad_tiles = masked_grad.reshape(patch_total, feature_depth, patch_extent, patch_extent)
    field_parts = collect_rims(edge_strips(inputs), neighbours, fold_flag)
    in_padded = padded_tiles(inputs, field_parts)
    pre_first = conv_forward(in_padded, w_first)
    value, slope = gelu_pair(pre_first)
    hidden = (value * water_indicator).astype(jnp.bfloat16)
    hidden_tiles = hidden.reshape(patch_total, feature_depth, patch_extent, patch_extent)
    hidden_parts = collect_rims(edge_strips(hidden_tiles), neighbours, fold_flag)
    hidden_padded = padded_tiles(hidden_tiles, hidden_parts)
    latter_linear_response = conv_forward(hidden_padded, w_second)
    prediction = (latter_linear_response * water_indicator).astype(jnp.bfloat16)[None]
    grad_parts = collect_rims(edge_strips(grad_tiles), neighbours, fold_flag)
    grad_padded = padded_tiles(grad_tiles, grad_parts)
    latter_kernel_slope = weight_grad(masked_grad, hidden_padded)
    back = conv_adjoint(grad_padded, w_second).reshape(
        patch_total, feature_depth, patch_extent, patch_extent
    )
    top_row = grad_padded[:, :, patch_extent + 1, :]
    correction = jnp.zeros((patch_total, feature_depth, patch_extent), jnp.float32)
    for shift_c in (-1, 0, 1):
        segment = top_row[:, :, 1 - shift_c : 1 - shift_c + patch_extent]
        correction = correction + jnp.einsum(
            "oi,toc->tic", w_second[7 - shift_c], segment, preferred_element_type=jnp.float32
        )
        correction = correction - jnp.einsum(
            "oi,toc->tic", w_second[1 + shift_c], segment, preferred_element_type=jnp.float32
        )
    flipped = (fold_flag == 1).astype(jnp.float32)[:, None, None]
    back = back.at[:, :, patch_extent - 1, :].add(correction * flipped)
    pre_grad = (back.reshape(patch_total, feature_depth, cells) * water_indicator * slope).astype(
        jnp.bfloat16
    )
    earlier_kernel_slope = weight_grad(pre_grad, in_padded)
    earlier_kernel_slope, latter_kernel_slope = lax.psum(
        (earlier_kernel_slope, latter_kernel_slope), ("space", "dp")
    )
    return (prediction, earlier_kernel_slope, latter_kernel_slope)


def solution(mesh):
    placed = (
        P("dp", "space", None, None),
        P("dp", "space", None, None),
        P("space", None),
        P("space", None),
        P("space"),
        P(),
        P(),
    )
    return jax.shard_map(
        body,
        mesh=mesh,
        in_specs=placed,
        out_specs=(P("dp", "space", None, None), P(), P()),
        check_vma=False,
    )
```

profile of v0, /device:TPU:1, one launch (start us, length us, event | category | flops | bytes accessed | tf_op | source)
XLA Modules:
  0.0 699.3 jit_solution(7048355584428669658)
XLA Ops:
  8.0 1.2 copy.238
  28.2 107.6 %all-gather.8.cloned.1.call-done = bf16[64,200,128]{2,1,0:T(8,128)(2,1)} async-done(((bf16[1,200,128]{2,1,0:T(8,128)(2,1)}), bf16[64,200,128]{2,1,0:T(8,128)(2,1)}) %all-gather.8.cloned.1.call-update) | async-done | bytes 3276816 | tf_op jit(solution)/shard_map/all_gather | solution.py:67
  135.8 1.0 constant_dynamic-slice_fusion.2
  139.2 121.1 %all-gather.4.cloned.1.call-done = bf16[64,200,128]{2,1,0:T(8,128)(2,1)} async-done(((bf16[1,200,128]{2,1,0:T(8,128)(2,1)}), bf16[64,200,128]{2,1,0:T(8,128)(2,1)}) %all-gather.4.cloned.1.call-update) | async-done | bytes 3276816 | tf_op jit(solution)/shard_map/all_gather | solution.py:67
  260.2 1.1 constant_dynamic-slice_fusion.18
  262.9 1.3 pad_maximum_fusion.7
  264.6 1.5 fusion.163
  271.2 1.2 fusion
  272.4 1.5 copy.252
  274.0 1.2 copy.253
  280.6 1.6 fusion.34
  282.2 1.3 copy.224
  284.5 2.0 fusion.23
  286.5 2.1 fusion.22
  290.5 1.0 fusion.19
  292.5 1.0 fusion.17
  295.4 109.5 %all-gather.6.cloned.1.call-done = bf16[64,200,128]{2,1,0:T(8,128)(2,1)} async-done(((bf16[1,200,128]{2,1,0:T(8,128)(2,1)}), bf16[64,200,128]{2,1,0:T(8,128)(2,1)}) %all-gather.6.cloned.1.call-update) | async-done | bytes 3276816 | tf_op jit(solution)/shard_map/all_gather | solution.py:67
  404.8 1.1 constant_dynamic-slice_fusion.10
  409.5 1.2 fusion.14
  411.4 1.2 fusion.13
  413.0 1.2 fusion.12
  414.2 1.2 fusion.11
  415.4 1.2 fusion.10
  416.6 1.2 fusion.9
  417.8 1.2 fusion.8
  419.0 1.2 fusion.7
  420.2 1.2 fusion.6
  421.4 1.4 convolution_add_fusion.13
  425.0 1.1 fusion.5
  426.1 262.5 %all-reduce.3.cloned.1.call-done = (f32[9,200,200]{2,1,0:T(8,128)}, f32[9,200,200]{2,1,0:T(8,128)}) async-done(((f32[9,200,200]{2,1,0:T(8,128)}, f32[9,200,200]{2,1,0:T(8,128)}), (f32[9,200,200]{2,1,0:T(8,128)}, f32[9,200,200]{2,1,0:T(8,128)})) %all-reduce.3.cloned.1.call-update) | async-done | bytes 2880016 | tf_op jit(solution)/shard_map/psum | solution.py:168
  688.6 3.0 copy.333
  691.6 1.2 copy.334
  (225 shorter events, 30.5 us)
Async XLA Ops:
  7.2 3.2 copy-start.13
  7.2 128.6 %all-gather.8.cloned.1.call-start = ((), (), s32[]{:S(2)}) async-start(), calls=%async_computation.2 | async-start | bytes 3328000 | tf_op jit(solution)/shard_map/all_gather | solution.py:67
  9.2 127.6 %copy-start.2 = (bf16[1,1,200,1024]{2,3,1,0:T(8,128)(2,1)}, bf16[1,1,200,1024]{2,3,1,0:T(8,128)(2,1)S(1)}, u32[]{:S(2)}) copy-start(bf16[1,1,200,1024]{2,3,1,0:T(8,128)(2,1)S(1)} %copy.238) | copy-start | bytes 1228804
  9.3 2.3 copy-start.31
  9.3 2.3 copy-start.30
  10.4 249.8 %all-gather.4.cloned.1.call-start = ((), (), s32[]{:S(2)}) async-start(), calls=%async_computation | async-start | bytes 3328000 | tf_op jit(solution)/shard_map/all_gather | solution.py:67
  10.6 127.8 %copy-start = (bf16[9,200,200]{2,1,0:T(8,128)(2,1)S(1)}, bf16[9,200,200]{2,1,0:T(8,128)(2,1)}, u32[]{:S(2)}) copy-start(bf16[9,200,200]{2,1,0:T(8,128)(2,1)} %param.17) | copy-start | bytes 2160004
  11.5 393.3 %all-gather.6.cloned.1.call-start = ((), (), s32[]{:S(2)}) async-start(), calls=%async_computation.1 | async-start | bytes 3328000 | tf_op jit(solution)/shard_map/all_gather | solution.py:67
  268.6 1.0 copy-start.3
  275.2 1.2 copy-start.29
  275.6 1.1 copy-start.12
  275.6 1.5 copy-start.11
  275.6 1.5 copy-start.9
  278.4 1.1 copy-start.5
  279.2 1.1 copy-start.23
  279.2 1.3 copy-start.28
  282.2 6.4 copy-start.10
  284.3 404.3 %all-reduce.3.cloned.1.call-start = ((), (), s32[]{:S(2)}) async-start(), calls=%async_computation.3 | async-start | bytes 7372800 | tf_op jit(solution)/shard_map/psum | solution.py:168
  286.5 4.0 copy-start.15
  289.6 2.9 copy-start.8
  290.5 2.9 copy-start.6
  291.5 2.9 copy-start.24
  407.9 6.2 copy-start.16
  408.5 1.0 copy-start.4
  411.1 6.7 copy-start.21
  411.1 7.9 %copy-start.19 = (bf16[1,200,32,32]{1,3,2,0:T(8,128)(2,1)}, bf16[1,200,32,32]{1,3,2,0:T(8,128)(2,1)S(1)}, u32[]{:S(2)}) copy-start(bf16[1,200,32,32]{1,3,2,0:T(8,128)(2,1)S(1)} %get-tuple-element.62) | copy-start | bytes 1228804
  411.1 9.1 %copy-start.17 = (bf16[1,200,32,32]{1,3,2,0:T(8,128)(2,1)}, bf16[1,200,32,32]{1,3,2,0:T(8,128)(2,1)S(1)}, u32[]{:S(2)}) copy-start(bf16[1,200,32,32]{1,3,2,0:T(8,128)(2,1)S(1)} %get-tuple-element.61) | copy-start | bytes 1228804
  413.0 2.4 copy-start.26
  421.4 1.4 copy-start.27
  423.1 1.1 copy-start.20
  423.9 1.1 copy-start.18
  688.6 3.0 copy-start.25
  (4 other events, 4.2 us)
Sparse Core Ops, SparseCore 0:
  12.0 123.7 all-gather.7
  139.8 120.3 all-gather.3
  284.4 120.3 all-gather.5
  421.5 267.0 all-reduce.2
where the time goes:
time: 702 us; the launch traced here: 699 us
  waiting for transfers between devices  601 us (86%)
  matrix products  35.5 us (5%)
  between operations  30.7 us (4%)
  local copies, waits for them, and re-layouts  27 us (4%)
    all_gather x3, waiting for transfers between devices, collect_rims(): lax.all_gather(strips, 'space', axis=0, tiled=True)  338 us
    psum x1, waiting for transfers between devices, body(): lax.psum((earlier_kernel_slope, latter_kernel_slope), ('space', 'dp'))  263 us
    dot_general x18, matrix products, weight_grad(): jnp.einsum('toc,tic->oi', grads, window(padded, k // 3 - 1, k % 3 - 1), p...  21.6 us
  transfers between devices with their start and end apart: 4, of which 4 were waited for; matrix products, arithmetic and copies ran while one was open for 3% of the time, Pallas kernels for 0%

commit v1 on v0

--- a/solution.py
+++ b/solution.py
@@ -66,6 +66,41 @@
 def collect_rims(strips, neighbours, fold_flag):
     found = strip_parts(lax.all_gather(strips, "space", axis=0, tiled=True), neighbours, fold_flag)
     return tuple((b for b in found))
+
+
+def collect_two_rims(first, second, neighbours, fold_flag):
+    depth = first.shape[1]
+    gathered = lax.all_gather(jnp.concatenate([first, second], axis=1), "space", axis=0, tiled=True)
+    return (
+        strip_parts(gathered[:, :depth], neighbours, fold_flag),
+        strip_parts(gathered[:, depth:], neighbours, fold_flag),
+    )
+
+
+REDUCE_AXES = ("space", "dp")
+
+
+def all_sum(x, mesh_sizes):
+    n = mesh_sizes
+    nbits = n.bit_length() - 1
+    idx = lax.axis_index(REDUCE_AXES)
+    buf = x.reshape(-1)
+    size = buf.shape[0]
+    padded = -(-size // n) * n
+    buf = jnp.pad(buf, (0, padded - size))
+    for b in range(nbits):
+        half = buf.shape[0] // 2
+        me = (idx >> b) & 1
+        pairs = [(i, i ^ (1 << b)) for i in range(n)]
+        keep = lax.dynamic_slice(buf, (me * half,), (half,))
+        send = lax.dynamic_slice(buf, ((1 - me) * half,), (half,))
+        buf = keep + lax.ppermute(send, REDUCE_AXES, pairs)
+    for b in reversed(range(nbits)):
+        me = (idx >> b) & 1
+        pairs = [(i, i ^ (1 << b)) for i in range(n)]
+        recv = lax.ppermute(buf, REDUCE_AXES, pairs)
+        buf = jnp.concatenate([jnp.where(me == 0, buf, recv), jnp.where(me == 0, recv, buf)])
+    return buf[:size].reshape(x.shape)
 
 
 def padded_tiles(field, parts):
@@ -133,7 +168,9 @@
     water_indicator = ocean.astype(jnp.float32)[:, None, :]
     masked_grad = (loss_sensitivity[0].astype(jnp.float32) * water_indicator).astype(jnp.bfloat16)
     grad_tiles = masked_grad.reshape(patch_total, feature_depth, patch_extent, patch_extent)
-    field_parts = collect_rims(edge_strips(inputs), neighbours, fold_flag)
+    field_parts, grad_parts = collect_two_rims(
+        edge_strips(inputs), edge_strips(grad_tiles), neighbours, fold_flag
+    )
     in_padded = padded_tiles(inputs, field_parts)
     pre_first = conv_forward(in_padded, w_first)
     value, slope = gelu_pair(pre_first)
@@ -143,7 +180,6 @@
     hidden_padded = padded_tiles(hidden_tiles, hidden_parts)
     latter_linear_response = conv_forward(hidden_padded, w_second)
     prediction = (latter_linear_response * water_indicator).astype(jnp.bfloat16)[None]
-    grad_parts = collect_rims(edge_strips(grad_tiles), neighbours, fold_flag)
     grad_padded = padded_tiles(grad_tiles, grad_parts)
     latter_kernel_slope = weight_grad(masked_grad, hidden_padded)
     back = conv_adjoint(grad_padded, w_second).reshape(
@@ -165,9 +201,9 @@
         jnp.bfloat16
     )
     earlier_kernel_slope = weight_grad(pre_grad, in_padded)
-    earlier_kernel_slope, latter_kernel_slope = lax.psum(
-        (earlier_kernel_slope, latter_kernel_slope), ("space", "dp")
-    )
+    devices = lax.psum(1, REDUCE_AXES)
+    earlier_kernel_slope = all_sum(earlier_kernel_slope, devices)
+    latter_kernel_slope = all_sum(latter_kernel_slope, devices)
     return (prediction, earlier_kernel_slope, latter_kernel_slope)
 
 

time: 702 us -> 496 us (0.71)
  waiting for transfers between devices: 601 us -> 267 us
  starting transfers between devices: 0.35 us -> 65.3 us
  local copies, waits for them, and re-layouts: 27 us -> 61.4 us
  other arithmetic: 5 us -> 23 us
    all_gather x3 -> x1, waiting for transfers between devices: 338 us -> 58.2 us  [collect_rims(): lax.all_gather(strips, 'space', axis=0, tiled=True)]
    psum x1 -> x0, waiting for transfers between devices: 263 us -> none  [body(): lax.psum((earlier_kernel_slope, latter_kernel_slope), ('space', 'dp'))]
    all_gather x0 -> x1, waiting for transfers between devices: none -> 124 us  [collect_two_rims(): lax.all_gather(jnp.concatenate([first, second], axis=1), 'space', axis=0,...]
    ppermute x0 -> x32, waiting for transfers between devices: none -> 83.8 us  [the longest x16 45.9 us: all_sum(): buf = keep + lax.ppermute(send, REDUCE_AXES, pairs)]
    ppermute x0 -> x32, starting transfers between devices: none -> 65.2 us  [the longest x16 35.1 us: all_sum(): recv = lax.ppermute(buf, REDUCE_AXES, pairs)]
    reshape x0 -> x4, local copies, waits for them, and re-layouts: none -> 14.8 us  [the longest x2 7.81 us: all_sum(): return buf[:size].reshape(x.shape)]
  transfers between devices with their start and end apart: 4 -> 34, of which waited for: 4 -> 29; matrix products, arithmetic and copies ran while one was open for 3% -> 8% of each run, Pallas kernels for 0% -> 0%
where the time goes in v1:
time: 496 us; the launch traced here: 489 us
  waiting for transfers between devices  267 us (54%)
  starting transfers between devices  65.3 us (13%)
  local copies, waits for them, and re-layouts  61.4 us (12%)
  matrix products  41.7 us (8%)
  between operations  31.1 us (6%)
  other arithmetic  23 us (5%)
    all_gather x1, waiting for transfers between devices, collect_two_rims(): lax.all_gather(jnp.concatenate([first, second], axis=1), 'space', axis=0,...  124 us
    all_gather x1, waiting for transfers between devices, collect_rims(): lax.all_gather(strips, 'space', axis=0, tiled=True)  58.2 us
    ppermute x16, waiting for transfers between devices, all_sum(): buf = keep + lax.ppermute(send, REDUCE_AXES, pairs)  45.9 us
    ppermute x16, waiting for transfers between devices, all_sum(): recv = lax.ppermute(buf, REDUCE_AXES, pairs)  37.9 us
    ppermute x16, starting transfers between devices, all_sum(): recv = lax.ppermute(buf, REDUCE_AXES, pairs)  35.1 us
    ppermute x16, starting transfers between devices, all_sum(): buf = keep + lax.ppermute(send, REDUCE_AXES, pairs)  30.1 us
    dot_general x18, matrix products, weight_grad(): jnp.einsum('toc,tic->oi', grads, window(padded, k // 3 - 1, k % 3 - 1), p...  19.4 us
    dot_general x18, matrix products, conv_forward(): jnp.einsum('oi,tic->toc', weights[k], window(padded, k // 3 - 1, k % 3 -...  13.9 us
  transfers between devices with their start and end apart: 34, of which 29 were waited for; matrix products, arithmetic and copies ran while one was open for 8% of the time, Pallas kernels for 0%

profile of v1, /device:TPU:1, one launch (start us, length us, event | category | flops | bytes accessed | tf_op | source)
XLA Modules:
  0.0 489.0 jit_solution(14665617906348196458)
XLA Ops:
  27.0 124.5 %all-gather.3.cloned.1.call-done = bf16[64,400,128]{2,1,0:T(8,128)(2,1)} async-done(((bf16[1,400,128]{2,1,0:T(8,128)(2,1)}), bf16[64,400,128]{2,1,0:T(8,128)(2,1)}) %all-gather.3.cloned.1.call-update) | async-done | bytes 6553616 | tf_op jit(solution)/shard_map/all_gather | solution.py:73
  151.5 5.2 %fusion.162 = (bf16[64,200,128]{2,1,0:T(8,128)(2,1)}, bf16[64,200,128]{2,1,0:T(8,128)(2,1)S(1)}) fusion(bf16[64,400,128]{2,1,0:T(8,128)(2,1)} %all-gather.3.cloned.1.call-done), kind=kLoop, calls=%fused_computation.352 | loop fusion | bytes 13107200 | tf_op jit(solution)/shard_map/slice | solution.py:76
  224.0 3.5 reshape.697
  228.7 4.3 collective-permute-start
  238.8 8.4 %collective-permute-done.1 = f32[90048]{0:T(1024)S(1)} collective-permute-done((f32[90048]{0:T(1024)S(1)}, f32[90048]{0:T(1024)S(1)}, u32[]{:S(2)}, u32[]{:S(2)}) %collective-permute-start.1) | collective-permute-done | bytes 360224 | tf_op jit(solution)/shard_map/ppermute | solution.py:97
  249.5 4.3 collective-permute-done.2
  255.1 4.9 collective-permute-done.3
  261.8 5.5 %collective-permute-done.4 = f32[11256]{0:T(1024)S(1)} collective-permute-done((f32[11256]{0:T(1024)S(1)}, f32[11256]{0:T(1024)S(1)}, u32[]{:S(2)}, u32[]{:S(2)}) %collective-permute-start.4) | collective-permute-done | bytes 45056 | tf_op jit(solution)/shard_map/ppermute | solution.py:97
  275.9 3.2 collective-permute-done.7
  280.1 3.1 collective-permute-done.8
  283.3 2.8 collective-permute-start.9
  292.2 5.5 %collective-permute-done.11 = f32[11256]{0:T(1024)S(1)} collective-permute-done((f32[11256]{0:T(1024)S(1)}, f32[11256]{0:T(1024)S(1)}, u32[]{:S(2)}, u32[]{:S(2)}) %collective-permute-start.11) | collective-permute-done | bytes 45056 | tf_op jit(solution)/shard_map/ppermute | solution.py:101
  298.5 58.2 %all-gather.5.cloned.1.call-done = bf16[64,200,128]{2,1,0:T(8,128)(2,1)} async-done(((bf16[1,200,128]{2,1,0:T(8,128)(2,1)}), bf16[64,200,128]{2,1,0:T(8,128)(2,1)}) %all-gather.5.cloned.1.call-update) | async-done | bytes 3276816 | tf_op jit(solution)/shard_map/all_gather | solution.py:67
  372.2 3.4 reshape.699
  375.9 4.4 collective-permute-start.16
  383.0 4.6 collective-permute-done.13
  387.7 4.6 collective-permute-done.17
  394.1 3.5 collective-permute-done.18
  397.8 2.7 collective-permute-start.19
  403.7 3.3 collective-permute-start.20
  407.2 3.5 collective-permute-start.15
  414.0 2.8 collective-permute-start.22
  419.3 3.0 collective-permute-done.23
  426.5 2.9 collective-permute-start.25
  429.5 3.9 reshape.698
  436.4 3.2 collective-permute-start.27
  440.0 3.3 collective-permute-done.27
  445.2 3.5 collective-permute-done.28
  449.4 4.7 collective-permute-done.29
  455.3 5.7 %collective-permute-done.30 = f32[90048]{0:T(1024)S(1)} collective-permute-done((f32[90048]{0:T(1024)S(1)}, f32[90048]{0:T(1024)S(1)}, u32[]{:S(2)}, u32[]{:S(2)}) %collective-permute-start.30) | collective-permute-done | bytes 360224 | tf_op jit(solution)/shard_map/ppermute | solution.py:101
  461.3 14.7 %collective-permute-start.31 = (f32[180096]{0:T(1024)S(1)}, f32[180096]{0:T(1024)S(1)}, u32[]{:S(2)}, u32[]{:S(2)}) collective-permute-start(f32[180096]{0:T(1024)S(1)} %pad_maximum_fusion.3), channel_id=1, source_target_pairs={{0,1},{1,0},{2,3},{3,2},{4,5},{5,4},{6,7},{7,6},{8,9},{9,8},{10,11... | collective-permute-start | bytes 2161160 | tf_op jit(solution)/shard_map/ppermute | solution.py:101
  478.1 3.9 reshape.700
  (380 shorter events, 142.8 us)
Async XLA Ops:
  7.2 144.3 %all-gather.3.cloned.1.call-start = ((), (), s32[]{:S(2)}) async-start(), calls=%async_computation | async-start | bytes 6656000 | tf_op jit(solution)/shard_map/all_gather | solution.py:73
  10.7 346.0 %all-gather.5.cloned.1.call-start = ((), (), s32[]{:S(2)}) async-start(), calls=%async_computation.1 | async-start | bytes 3328000 | tf_op jit(solution)/shard_map/all_gather | solution.py:67
  228.7 6.5 %collective-permute-start = (f32[180096]{0:T(1024)}, f32[180096]{0:T(1024)}, u32[]{:S(2)}, u32[]{:S(2)}) collective-permute-start(f32[180096]{0:T(1024)} %pad_dynamic-slice_fusion.2), channel_id=1, source_target_pairs={{0,1},{1,0},{2,3},{3,2},{4,5},{5,4},{6,7},{7,6},{8,9},{9,8},{10,11... | collective-permute-start | bytes 2161160 | tf_op jit(solution)/shard_map/ppermute | solution.py:97
  237.6 9.7 %collective-permute-start.1 = (f32[90048]{0:T(1024)S(1)}, f32[90048]{0:T(1024)S(1)}, u32[]{:S(2)}, u32[]{:S(2)}) collective-permute-start(f32[90048]{0:T(1024)S(1)} %dynamic_slice.99), channel_id=1, source_target_pairs={{0,2},{1,3},{2,0},{3,1},{4,6},{5,7},{6,4},{7,5},{8,10},{9,11},{10,... | collective-permute-start | bytes 1080584 | tf_op jit(solution)/shard_map/ppermute | solution.py:97
  248.6 5.3 %collective-permute-start.2 = (f32[45024]{0:T(1024)S(1)}, f32[45024]{0:T(1024)S(1)}, u32[]{:S(2)}, u32[]{:S(2)}) collective-permute-start(f32[45024]{0:T(1024)S(1)} %dynamic_slice.101), channel_id=1, source_target_pairs={{0,4},{1,5},{2,6},{3,7},{4,0},{5,1},{6,2},{7,3},{8,12},{9,13},{10,... | collective-permute-start | bytes 540296 | tf_op jit(solution)/shard_map/ppermute | solution.py:97
  254.1 5.9 %collective-permute-start.3 = (f32[22512]{0:T(1024)S(1)}, f32[22512]{0:T(1024)S(1)}, u32[]{:S(2)}, u32[]{:S(2)}) collective-permute-start(f32[22512]{0:T(1024)S(1)} %dynamic_slice.103), channel_id=1, source_target_pairs={{0,8},{1,9},{2,10},{3,11},{4,12},{5,13},{6,14},{7,15},{8,0},{9,1},... | collective-permute-start | bytes 270152 | tf_op jit(solution)/shard_map/ppermute | solution.py:97
  260.2 7.2 %collective-permute-start.4 = (f32[11256]{0:T(1024)S(1)}, f32[11256]{0:T(1024)S(1)}, u32[]{:S(2)}, u32[]{:S(2)}) collective-permute-start(f32[11256]{0:T(1024)S(1)} %dynamic_slice.105), channel_id=1, source_target_pairs={{0,16},{1,17},{2,18},{3,19},{4,20},{5,21},{6,22},{7,23},{8,24},{9,... | collective-permute-start | bytes 135080 | tf_op jit(solution)/shard_map/ppermute | solution.py:97
  267.5 3.1 collective-permute-start.5
  270.8 4.1 collective-permute-start.6
  275.0 4.0 collective-permute-start.7
  279.1 4.0 collective-permute-start.8
  283.3 4.1 collective-permute-start.9
  287.5 3.1 collective-permute-start.10
  290.7 6.9 %collective-permute-start.11 = (f32[11256]{0:T(1024)S(1)}, f32[11256]{0:T(1024)S(1)}, u32[]{:S(2)}, u32[]{:S(2)}) collective-permute-start(f32[11256]{0:T(1024)S(1)} %pad_maximum_fusion.20), channel_id=1, source_target_pairs={{0,16},{1,17},{2,18},{3,19},{4,20},{5,21},{6,22},{7,23},{8,24},{9,... | collective-permute-start | bytes 135080 | tf_op jit(solution)/shard_map/ppermute | solution.py:101
  298.5 81.8 %collective-permute-start.12 = (f32[22512]{0:T(1024)}, f32[22512]{0:T(1024)}, u32[]{:S(2)}, u32[]{:S(2)}) collective-permute-start(f32[22512]{0:T(1024)} %pad_maximum_fusion.17), channel_id=1, source_target_pairs={{0,8},{1,9},{2,10},{3,11},{4,12},{5,13},{6,14},{7,15},{8,0},{9,1},... | collective-permute-start | bytes 270152 | tf_op jit(solution)/shard_map/ppermute | solution.py:101
  375.9 6.2 %collective-permute-start.16 = (f32[180096]{0:T(1024)S(1)}, f32[180096]{0:T(1024)S(1)}, u32[]{:S(2)}, u32[]{:S(2)}) collective-permute-start(f32[180096]{0:T(1024)S(1)} %pad_dynamic-slice_fusion), channel_id=1, source_target_pairs={{0,1},{1,0},{2,3},{3,2},{4,5},{5,4},{6,7},{7,6},{8,9},{9,8},{10,11... | collective-permute-start | bytes 2161160 | tf_op jit(solution)/shard_map/ppermute | solution.py:97
  381.4 6.2 %collective-permute-start.13 = (f32[45024]{0:T(1024)S(1)}, f32[45024]{0:T(1024)S(1)}, u32[]{:S(2)}, u32[]{:S(2)}) collective-permute-start(f32[45024]{0:T(1024)S(1)} %pad_maximum_fusion.15), channel_id=1, source_target_pairs={{0,4},{1,5},{2,6},{3,7},{4,0},{5,1},{6,2},{7,3},{8,12},{9,13},{10,... | collective-permute-start | bytes 540296 | tf_op jit(solution)/shard_map/ppermute | solution.py:101
  382.6 9.7 %collective-permute-start.17 = (f32[90048]{0:T(1024)S(1)}, f32[90048]{0:T(1024)S(1)}, u32[]{:S(2)}, u32[]{:S(2)}) collective-permute-start(f32[90048]{0:T(1024)S(1)} %dynamic_slice.115), channel_id=1, source_target_pairs={{0,2},{1,3},{2,0},{3,1},{4,6},{5,7},{6,4},{7,5},{8,10},{9,11},{10,... | collective-permute-start | bytes 1080584 | tf_op jit(solution)/shard_map/ppermute | solution.py:97
  392.6 5.0 %collective-permute-start.18 = (f32[45024]{0:T(1024)S(1)}, f32[45024]{0:T(1024)S(1)}, u32[]{:S(2)}, u32[]{:S(2)}) collective-permute-start(f32[45024]{0:T(1024)S(1)} %dynamic_slice.117), channel_id=1, source_target_pairs={{0,4},{1,5},{2,6},{3,7},{4,0},{5,1},{6,2},{7,3},{8,12},{9,13},{10,... | collective-permute-start | bytes 540296 | tf_op jit(solution)/shard_map/ppermute | solution.py:97
  393.7 8.6 %collective-permute-start.14 = (f32[90048]{0:T(1024)S(1)}, f32[90048]{0:T(1024)S(1)}, u32[]{:S(2)}, u32[]{:S(2)}) collective-permute-start(f32[90048]{0:T(1024)S(1)} %pad_maximum_fusion.13), channel_id=1, source_target_pairs={{0,2},{1,3},{2,0},{3,1},{4,6},{5,7},{6,4},{7,5},{8,10},{9,11},{10,... | collective-permute-start | bytes 1080584 | tf_op jit(solution)/shard_map/ppermute | solution.py:101
  397.8 5.7 %collective-permute-start.19 = (f32[22512]{0:T(1024)S(1)}, f32[22512]{0:T(1024)S(1)}, u32[]{:S(2)}, u32[]{:S(2)}) collective-permute-start(f32[22512]{0:T(1024)S(1)} %dynamic_slice.119), channel_id=1, source_target_pairs={{0,8},{1,9},{2,10},{3,11},{4,12},{5,13},{6,14},{7,15},{8,0},{9,1},... | collective-permute-start | bytes 270152 | tf_op jit(solution)/shard_map/ppermute | solution.py:97
  403.7 7.0 %collective-permute-start.20 = (f32[11256]{0:T(1024)S(1)}, f32[11256]{0:T(1024)S(1)}, u32[]{:S(2)}, u32[]{:S(2)}) collective-permute-start(f32[11256]{0:T(1024)S(1)} %dynamic_slice.121), channel_id=1, source_target_pairs={{0,16},{1,17},{2,18},{3,19},{4,20},{5,21},{6,22},{7,23},{8,24},{9,... | collective-permute-start | bytes 135080 | tf_op jit(solution)/shard_map/ppermute | solution.py:97
  407.2 16.3 %collective-permute-start.15 = (f32[180096]{0:T(1024)S(1)}, f32[180096]{0:T(1024)}, u32[]{:S(2)}, u32[]{:S(2)}) collective-permute-start(f32[180096]{0:T(1024)S(1)} %pad_maximum_fusion.2), channel_id=1, source_target_pairs={{0,1},{1,0},{2,3},{3,2},{4,5},{5,4},{6,7},{7,6},{8,9},{9,8},{10,11... | collective-permute-start | bytes 2161160 | tf_op jit(solution)/shard_map/ppermute | solution.py:101
  414.0 4.1 collective-permute-start.22
  418.3 4.0 collective-permute-start.23
  422.4 4.0 collective-permute-start.24
  426.5 6.9 %collective-permute-start.25 = (f32[2814]{0:T(1024)S(1)}, f32[2814]{0:T(1024)S(1)}, u32[]{:S(2)}, u32[]{:S(2)}) collective-permute-start(f32[2814]{0:T(1024)S(1)} %pad_maximum_fusion.27), channel_id=1, source_target_pairs={{0,64},{1,65},{2,66},{3,67},{4,68},{5,69},{6,70},{7,71},{8,72},{9,... | collective-permute-start | bytes 33776 | tf_op jit(solution)/shard_map/ppermute | solution.py:101
  436.4 6.8 %collective-permute-start.27 = (f32[11256]{0:T(1024)S(1)}, f32[11256]{0:T(1024)S(1)}, u32[]{:S(2)}, u32[]{:S(2)}) collective-permute-start(f32[11256]{0:T(1024)S(1)} %pad_maximum_fusion.21), channel_id=1, source_target_pairs={{0,16},{1,17},{2,18},{3,19},{4,20},{5,21},{6,22},{7,23},{8,24},{9,... | collective-permute-start | bytes 135080 | tf_op jit(solution)/shard_map/ppermute | solution.py:101
  443.4 5.3 %collective-permute-start.28 = (f32[22512]{0:T(1024)S(1)}, f32[22512]{0:T(1024)S(1)}, u32[]{:S(2)}, u32[]{:S(2)}) collective-permute-start(f32[22512]{0:T(1024)S(1)} %pad_maximum_fusion.18), channel_id=1, source_target_pairs={{0,8},{1,9},{2,10},{3,11},{4,12},{5,13},{6,14},{7,15},{8,0},{9,1},... | collective-permute-start | bytes 270152 | tf_op jit(solution)/shard_map/ppermute | solution.py:101
  448.9 5.2 %collective-permute-start.29 = (f32[45024]{0:T(1024)S(1)}, f32[45024]{0:T(1024)S(1)}, u32[]{:S(2)}, u32[]{:S(2)}) collective-permute-start(f32[45024]{0:T(1024)S(1)} %pad_maximum_fusion.16), channel_id=1, source_target_pairs={{0,4},{1,5},{2,6},{3,7},{4,0},{5,1},{6,2},{7,3},{8,12},{9,13},{10,... | collective-permute-start | bytes 540296 | tf_op jit(solution)/shard_map/ppermute | solution.py:101
  454.3 6.7 %collective-permute-start.30 = (f32[90048]{0:T(1024)S(1)}, f32[90048]{0:T(1024)S(1)}, u32[]{:S(2)}, u32[]{:S(2)}) collective-permute-start(f32[90048]{0:T(1024)S(1)} %pad_maximum_fusion.14), channel_id=1, source_target_pairs={{0,2},{1,3},{2,0},{3,1},{4,6},{5,7},{6,4},{7,5},{8,10},{9,11},{10,... | collective-permute-start | bytes 1080584 | tf_op jit(solution)/shard_map/ppermute | solution.py:101
  461.3 16.5 %collective-permute-start.31 = (f32[180096]{0:T(1024)S(1)}, f32[180096]{0:T(1024)S(1)}, u32[]{:S(2)}, u32[]{:S(2)}) collective-permute-start(f32[180096]{0:T(1024)S(1)} %pad_maximum_fusion.3), channel_id=1, source_target_pairs={{0,1},{1,0},{2,3},{3,2},{4,5},{5,4},{6,7},{7,6},{8,9},{9,8},{10,11... | collective-permute-start | bytes 2161160 | tf_op jit(solution)/shard_map/ppermute | solution.py:101
  (45 other events, 223.7 us)
Sparse Core Ops, SparseCore 0:
  12.2 139.2 all-gather.2
  239.0 117.6 all-gather.4

commit v2 on v1

--- a/solution.py
+++ b/solution.py
@@ -80,27 +80,39 @@
 REDUCE_AXES = ("space", "dp")
 
 
-def all_sum(x, mesh_sizes):
-    n = mesh_sizes
-    nbits = n.bit_length() - 1
+def all_sum(x, devices):
+    digits = 0
+    while 4 ** digits < devices:
+        digits += 1
     idx = lax.axis_index(REDUCE_AXES)
-    buf = x.reshape(-1)
-    size = buf.shape[0]
-    padded = -(-size // n) * n
-    buf = jnp.pad(buf, (0, padded - size))
-    for b in range(nbits):
-        half = buf.shape[0] // 2
-        me = (idx >> b) & 1
-        pairs = [(i, i ^ (1 << b)) for i in range(n)]
-        keep = lax.dynamic_slice(buf, (me * half,), (half,))
-        send = lax.dynamic_slice(buf, ((1 - me) * half,), (half,))
-        buf = keep + lax.ppermute(send, REDUCE_AXES, pairs)
-    for b in reversed(range(nbits)):
-        me = (idx >> b) & 1
-        pairs = [(i, i ^ (1 << b)) for i in range(n)]
-        recv = lax.ppermute(buf, REDUCE_AXES, pairs)
-        buf = jnp.concatenate([jnp.where(me == 0, buf, recv), jnp.where(me == 0, recv, buf)])
-    return buf[:size].reshape(x.shape)
+    buf = x.reshape(-1, x.shape[-1])
+    rows = buf.shape[0]
+    unit = devices * 8
+    buf = jnp.pad(buf, ((0, -(-rows // unit) * unit - rows), (0, 0)))
+    for g in range(digits):
+        quarter = buf.shape[0] // 4
+        mine = (idx >> (2 * g)) & 3
+        total = lax.dynamic_slice_in_dim(buf, mine * quarter, quarter, axis=0)
+        for j in (1, 2, 3):
+            pairs = [(i, i ^ (j << (2 * g))) for i in range(devices)]
+            piece = lax.dynamic_slice_in_dim(buf, (mine ^ j) * quarter, quarter, axis=0)
+            total = total + lax.ppermute(piece, REDUCE_AXES, pairs)
+        buf = total
+    for g in reversed(range(digits)):
+        mine = (idx >> (2 * g)) & 3
+        got = [buf]
+        for j in (1, 2, 3):
+            pairs = [(i, i ^ (j << (2 * g))) for i in range(devices)]
+            got.append(lax.ppermute(buf, REDUCE_AXES, pairs))
+        parts = []
+        for p in range(4):
+            rel = mine ^ p
+            part = got[3]
+            for j in (2, 1, 0):
+                part = jnp.where(rel == j, got[j], part)
+            parts.append(part)
+        buf = jnp.concatenate(parts, axis=0)
+    return buf[:rows].reshape(x.shape)
 
 
 def padded_tiles(field, parts):

time: 496 us -> 559 us (1.13)
  starting transfers between devices: 65.3 us -> 102 us
  local copies, waits for them, and re-layouts: 61.4 us -> 73.3 us
  other arithmetic: 23 us -> 34.3 us
  matrix products: 41.7 us -> 34.2 us
  waiting for transfers between devices: 267 us -> 274 us
    ppermute x32 -> x48, waiting for transfers between devices: 83.8 us -> 150 us  [the longest x24 79.7 us: all_sum(): total = total + lax.ppermute(piece, REDUCE_AXES, pairs)]
    all_gather x1, waiting for transfers between devices: 58.2 us -> 0.02 us  [collect_rims(): lax.all_gather(strips, 'space', axis=0, tiled=True)]
    ppermute x32 -> x48, starting transfers between devices: 65.2 us -> 102 us  [the longest x24 60.1 us: all_sum(): got.append(lax.ppermute(buf, REDUCE_AXES, pairs))]
    unnamed x116, local copies, waits for them, and re-layouts: 12.8 us -> 29 us
    reshape x4 -> x0, local copies, waits for them, and re-layouts: 14.8 us -> none  [the longest x2 7.81 us: all_sum(): return buf[:size].reshape(x.shape)]
    dot_general x18, matrix products: 19.4 us -> 11.5 us  [weight_grad(): jnp.einsum('toc,tic->oi', grads, window(padded, k // 3 - 1, k % 3 - 1), p...]
    mul x18, other arithmetic: 2.77 us -> 9.61 us  [pick(): jnp.take(piece, jnp.clip(index, 0, amount - 1), axis=0)]
  transfers between devices with their start and end apart: 34 -> 50, of which waited for: 29 -> 29; matrix products, arithmetic and copies ran while one was open for 8% -> 3% of each run, Pallas kernels for 0% -> 0%
where the time goes in v2:
time: 559 us; the launch traced here: 550 us
  waiting for transfers between devices  274 us (49%)
  starting transfers between devices  102 us (18%)
  local copies, waits for them, and re-layouts  73.3 us (13%)
  other arithmetic  34.3 us (6%)
  matrix products  34.2 us (6%)
  between operations  32.3 us (6%)
    all_gather x1, waiting for transfers between devices, collect_two_rims(): lax.all_gather(jnp.concatenate([first, second], axis=1), 'space', axis=0,...  123 us
    ppermute x24, waiting for transfers between devices, all_sum(): total = total + lax.ppermute(piece, REDUCE_AXES, pairs)  79.7 us
    ppermute x24, waiting for transfers between devices, all_sum(): got.append(lax.ppermute(buf, REDUCE_AXES, pairs))  70.6 us
    ppermute x24, starting transfers between devices, all_sum(): got.append(lax.ppermute(buf, REDUCE_AXES, pairs))  60.1 us
    ppermute x24, starting transfers between devices, all_sum(): total = total + lax.ppermute(piece, REDUCE_AXES, pairs)  42 us
    unnamed x116, local copies, waits for them, and re-layouts  29 us
    dot_general x18, matrix products, conv_forward(): jnp.einsum('oi,tic->toc', weights[k], window(padded, k // 3 - 1, k % 3 -...  12 us
    dot_general x18, matrix products, weight_grad(): jnp.einsum('toc,tic->oi', grads, window(padded, k // 3 - 1, k % 3 - 1), p...  11.5 us
  transfers between devices with their start and end apart: 50, of which 29 were waited for; matrix products, arithmetic and copies ran while one was open for 3% of the time, Pallas kernels for 0%

profile of v2, /device:TPU:1, one launch (start us, length us, event | category | flops | bytes accessed | tf_op | source)
XLA Modules:
  0.0 550.0 jit_solution(7449781949836302498)
XLA Ops:
  28.2 123.3 %all-gather.3.cloned.1.call-done = bf16[64,400,128]{2,1,0:T(8,128)(2,1)} async-done(((bf16[1,400,128]{2,1,0:T(8,128)(2,1)}), bf16[64,400,128]{2,1,0:T(8,128)(2,1)}) %all-gather.3.cloned.1.call-update) | async-done | bytes 6553616 | tf_op jit(solution)/shard_map/all_gather | solution.py:73
  151.5 5.1 fusion.172
  234.6 4.3 collective-permute-start
  240.9 12.1 %collective-permute-done.1 = f32[512,200]{1,0:T(8,128)} collective-permute-done((f32[512,200]{1,0:T(8,128)}, f32[512,200]{1,0:T(8,128)}, u32[]{:S(2)}, u32[]{:S(2)}) %collective-permute-start.1) | collective-permute-done | bytes 409632 | tf_op jit(solution)/shard_map/ppermute | solution.py:99
  253.0 11.5 %collective-permute-done.2 = f32[512,200]{1,0:T(8,128)} collective-permute-done((f32[512,200]{1,0:T(8,128)}, f32[512,200]{1,0:T(8,128)}, u32[]{:S(2)}, u32[]{:S(2)}) %collective-permute-start.2) | collective-permute-done | bytes 409632 | tf_op jit(solution)/shard_map/ppermute | solution.py:99
  269.8 3.1 collective-permute-done.3
  272.9 5.9 %collective-permute-done.4 = f32[128,200]{1,0:T(8,128)S(1)} collective-permute-done((f32[128,200]{1,0:T(8,128)S(1)}, f32[128,200]{1,0:T(8,128)S(1)}, u32[]{:S(2)}, u32[]{:S(2)}) %collective-permute-start.4) | collective-permute-done | bytes 102432 | tf_op jit(solution)/shard_map/ppermute | solution.py:99
  285.6 4.9 collective-permute-done.8
  290.6 5.0 collective-permute-start.11
  305.3 3.5 collective-permute-done.14
  308.9 3.0 collective-permute-start.15
  311.9 3.6 collective-permute-start.17
  315.7 3.9 collective-permute-done.17
  319.7 3.8 collective-permute-start.18
  328.9 3.3 collective-permute-done.20
  332.4 10.9 %collective-permute-start.21 = (f32[512,200]{1,0:T(8,128)S(1)}, f32[512,200]{1,0:T(8,128)S(1)}, u32[]{:S(2)}, u32[]{:S(2)}) collective-permute-start(f32[512,200]{1,0:T(8,128)S(1)} %pad_maximum_fusion.15), channel_id=1, source_target_pairs={{0,1},{1,0},{2,3},{3,2},{4,5},{5,4},{6,7},{7,6},{8,9},{9,8},{10,11... | collective-permute-start | bytes 1228808 | tf_op jit(solution)/shard_map/ppermute | solution.py:106
  345.6 10.7 %collective-permute-done.22 = f32[512,200]{1,0:T(8,128)S(1)} collective-permute-done((f32[512,200]{1,0:T(8,128)S(1)}, f32[512,200]{1,0:T(8,128)S(1)}, u32[]{:S(2)}, u32[]{:S(2)}) %collective-permute-start.22) | collective-permute-done | bytes 409632 | tf_op jit(solution)/shard_map/ppermute | solution.py:106
  356.3 11.8 %collective-permute-done.23 = f32[512,200]{1,0:T(8,128)S(1)} collective-permute-done((f32[512,200]{1,0:T(8,128)S(1)}, f32[512,200]{1,0:T(8,128)S(1)}, u32[]{:S(2)}, u32[]{:S(2)}) %collective-permute-start.23) | collective-permute-done | bytes 409632 | tf_op jit(solution)/shard_map/ppermute | solution.py:106
  418.6 9.3 %collective-permute-done.25 = f32[512,200]{1,0:T(8,128)S(1)} collective-permute-done((f32[512,200]{1,0:T(8,128)S(1)}, f32[512,200]{1,0:T(8,128)S(1)}, u32[]{:S(2)}, u32[]{:S(2)}) %collective-permute-start.25) | collective-permute-done | bytes 409632 | tf_op jit(solution)/shard_map/ppermute | solution.py:99
  428.0 11.8 %collective-permute-done.26 = f32[512,200]{1,0:T(8,128)S(1)} collective-permute-done((f32[512,200]{1,0:T(8,128)S(1)}, f32[512,200]{1,0:T(8,128)S(1)}, u32[]{:S(2)}, u32[]{:S(2)}) %collective-permute-start.26) | collective-permute-done | bytes 409632 | tf_op jit(solution)/shard_map/ppermute | solution.py:99
  445.1 3.9 collective-permute-done.27
  449.0 5.1 collective-permute-done.29
  461.5 5.4 collective-permute-done.32
  469.7 3.0 collective-permute-start.35
  473.0 3.0 collective-permute-done.35
  482.0 3.8 collective-permute-done.38
  488.2 4.3 collective-permute-start.41
  492.8 3.3 collective-permute-done.41
  501.5 5.3 collective-permute-done.43
  506.9 9.5 %collective-permute-start.45 = (f32[512,200]{1,0:T(8,128)S(1)}, f32[512,200]{1,0:T(8,128)S(1)}, u32[]{:S(2)}, u32[]{:S(2)}) collective-permute-start(f32[512,200]{1,0:T(8,128)S(1)} %pad_maximum_fusion.16), channel_id=1, source_target_pairs={{0,1},{1,0},{2,3},{3,2},{4,5},{5,4},{6,7},{7,6},{8,9},{9,8},{10,11... | collective-permute-start | bytes 1228808 | tf_op jit(solution)/shard_map/ppermute | solution.py:106
  519.6 10.2 %collective-permute-done.46 = f32[512,200]{1,0:T(8,128)S(1)} collective-permute-done((f32[512,200]{1,0:T(8,128)S(1)}, f32[512,200]{1,0:T(8,128)S(1)}, u32[]{:S(2)}, u32[]{:S(2)}) %collective-permute-start.46) | collective-permute-done | bytes 409632 | tf_op jit(solution)/shard_map/ppermute | solution.py:106
  529.8 11.5 %collective-permute-done.47 = f32[512,200]{1,0:T(8,128)S(1)} collective-permute-done((f32[512,200]{1,0:T(8,128)S(1)}, f32[512,200]{1,0:T(8,128)S(1)}, u32[]{:S(2)}, u32[]{:S(2)}) %collective-permute-start.47) | collective-permute-done | bytes 409632 | tf_op jit(solution)/shard_map/ppermute | solution.py:106
  (382 shorter events, 198.3 us)
Async XLA Ops:
  7.2 144.3 %all-gather.3.cloned.1.call-start = ((), (), s32[]{:S(2)}) async-start(), calls=%async_computation | async-start | bytes 6656000 | tf_op jit(solution)/shard_map/all_gather | solution.py:73
  10.8 360.8 %all-gather.5.cloned.1.call-start = ((), (), s32[]{:S(2)}) async-start(), calls=%async_computation.1 | async-start | bytes 3328000 | tf_op jit(solution)/shard_map/all_gather | solution.py:67
  238.9 14.2 %collective-permute-start.1 = (f32[512,200]{1,0:T(8,128)}, f32[512,200]{1,0:T(8,128)}, u32[]{:S(2)}, u32[]{:S(2)}) collective-permute-start(f32[512,200]{1,0:T(8,128)} %get-tuple-element.65), channel_id=1, source_target_pairs={{0,2},{1,3},{2,0},{3,1},{4,6},{5,7},{6,4},{7,5},{8,10},{9,11},{10,... | collective-permute-start | bytes 1228808 | tf_op jit(solution)/shard_map/ppermute | solution.py:99
  239.2 25.4 %collective-permute-start.2 = (f32[512,200]{1,0:T(8,128)}, f32[512,200]{1,0:T(8,128)}, u32[]{:S(2)}, u32[]{:S(2)}) collective-permute-start(f32[512,200]{1,0:T(8,128)} %get-tuple-element.66), channel_id=1, source_target_pairs={{0,3},{1,2},{2,1},{3,0},{4,7},{5,6},{6,5},{7,4},{8,11},{9,10},{10,... | collective-permute-start | bytes 1228808 | tf_op jit(solution)/shard_map/ppermute | solution.py:99
  266.1 6.8 %collective-permute-start.3 = (f32[128,200]{1,0:T(8,128)S(1)}, f32[128,200]{1,0:T(8,128)S(1)}, u32[]{:S(2)}, u32[]{:S(2)}) collective-permute-start(f32[128,200]{1,0:T(8,128)S(1)} %get-tuple-element.104), channel_id=1, source_target_pairs={{0,4},{1,5},{2,6},{3,7},{4,0},{5,1},{6,2},{7,3},{8,12},{9,13},{10,... | collective-permute-start | bytes 307208 | tf_op jit(solution)/shard_map/ppermute | solution.py:99
  267.4 11.4 %collective-permute-start.4 = (f32[128,200]{1,0:T(8,128)S(1)}, f32[128,200]{1,0:T(8,128)S(1)}, u32[]{:S(2)}, u32[]{:S(2)}) collective-permute-start(f32[128,200]{1,0:T(8,128)S(1)} %get-tuple-element.106), channel_id=1, source_target_pairs={{0,8},{1,9},{2,10},{3,11},{4,12},{5,13},{6,14},{7,15},{8,0},{9,1},... | collective-permute-start | bytes 307208 | tf_op jit(solution)/shard_map/ppermute | solution.py:99
  269.2 9.6 %collective-permute-start.5 = (f32[128,200]{1,0:T(8,128)S(1)}, f32[128,200]{1,0:T(8,128)S(1)}, u32[]{:S(2)}, u32[]{:S(2)}) collective-permute-start(f32[128,200]{1,0:T(8,128)S(1)} %get-tuple-element.105), channel_id=1, source_target_pairs={{0,12},{1,13},{2,14},{3,15},{4,8},{5,9},{6,10},{7,11},{8,4},{9,5},... | collective-permute-start | bytes 307208 | tf_op jit(solution)/shard_map/ppermute | solution.py:99
  278.9 6.8 %collective-permute-start.6 = (f32[32,200]{1,0:T(8,128)S(1)}, f32[32,200]{1,0:T(8,128)S(1)}, u32[]{:S(2)}, u32[]{:S(2)}) collective-permute-start(f32[32,200]{1,0:T(8,128)S(1)} %get-tuple-element.136), channel_id=1, source_target_pairs={{0,16},{1,17},{2,18},{3,19},{4,20},{5,21},{6,22},{7,23},{8,24},{9,... | collective-permute-start | bytes 76808 | tf_op jit(solution)/shard_map/ppermute | solution.py:99
  282.8 7.7 %collective-permute-start.8 = (f32[32,200]{1,0:T(8,128)S(1)}, f32[32,200]{1,0:T(8,128)S(1)}, u32[]{:S(2)}, u32[]{:S(2)}) collective-permute-start(f32[32,200]{1,0:T(8,128)S(1)} %get-tuple-element.137), channel_id=1, source_target_pairs={{0,48},{1,49},{2,50},{3,51},{4,52},{5,53},{6,54},{7,55},{8,56},{9,... | collective-permute-start | bytes 76808 | tf_op jit(solution)/shard_map/ppermute | solution.py:99
  290.6 6.5 %collective-permute-start.11 = (f32[8,200]{1,0:T(8,128)S(1)}, f32[8,200]{1,0:T(8,128)S(1)}, u32[]{:S(2)}, u32[]{:S(2)}) collective-permute-start(f32[8,200]{1,0:T(8,128)S(1)} %get-tuple-element.151), channel_id=1, source_target_pairs={{0,192},{1,193},{2,194},{3,195},{4,196},{5,197},{6,198},{7,199},{8... | collective-permute-start | bytes 19208 | tf_op jit(solution)/shard_map/ppermute | solution.py:99
  302.5 6.4 %collective-permute-start.14 = (f32[8,200]{1,0:T(8,128)S(1)}, f32[8,200]{1,0:T(8,128)S(1)}, u32[]{:S(2)}, u32[]{:S(2)}) collective-permute-start(f32[8,200]{1,0:T(8,128)S(1)} %fusion.142), channel_id=1, source_target_pairs={{0,192},{1,193},{2,194},{3,195},{4,196},{5,197},{6,198},{7,199},{8... | collective-permute-start | bytes 19208 | tf_op jit(solution)/shard_map/ppermute | solution.py:106
  308.9 6.8 %collective-permute-start.15 = (f32[32,200]{1,0:T(8,128)S(1)}, f32[32,200]{1,0:T(8,128)S(1)}, u32[]{:S(2)}, u32[]{:S(2)}) collective-permute-start(f32[32,200]{1,0:T(8,128)S(1)} %pad_maximum_fusion.20), channel_id=1, source_target_pairs={{0,16},{1,17},{2,18},{3,19},{4,20},{5,21},{6,22},{7,23},{8,24},{9,... | collective-permute-start | bytes 76808 | tf_op jit(solution)/shard_map/ppermute | solution.py:106
  311.9 7.7 %collective-permute-start.17 = (f32[32,200]{1,0:T(8,128)S(1)}, f32[32,200]{1,0:T(8,128)S(1)}, u32[]{:S(2)}, u32[]{:S(2)}) collective-permute-start(f32[32,200]{1,0:T(8,128)S(1)} %pad_maximum_fusion.20), channel_id=1, source_target_pairs={{0,48},{1,49},{2,50},{3,51},{4,52},{5,53},{6,54},{7,55},{8,56},{9,... | collective-permute-start | bytes 76808 | tf_op jit(solution)/shard_map/ppermute | solution.py:106
  319.7 6.7 %collective-permute-start.18 = (f32[128,200]{1,0:T(8,128)S(1)}, f32[128,200]{1,0:T(8,128)S(1)}, u32[]{:S(2)}, u32[]{:S(2)}) collective-permute-start(f32[128,200]{1,0:T(8,128)S(1)} %pad_maximum_fusion.17), channel_id=1, source_target_pairs={{0,4},{1,5},{2,6},{3,7},{4,0},{5,1},{6,2},{7,3},{8,12},{9,13},{10,... | collective-permute-start | bytes 307208 | tf_op jit(solution)/shard_map/ppermute | solution.py:106
  324.9 7.3 %collective-permute-start.20 = (f32[128,200]{1,0:T(8,128)S(1)}, f32[128,200]{1,0:T(8,128)S(1)}, u32[]{:S(2)}, u32[]{:S(2)}) collective-permute-start(f32[128,200]{1,0:T(8,128)S(1)} %pad_maximum_fusion.17), channel_id=1, source_target_pairs={{0,12},{1,13},{2,14},{3,15},{4,8},{5,9},{6,10},{7,11},{8,4},{9,5},... | collective-permute-start | bytes 307208 | tf_op jit(solution)/shard_map/ppermute | solution.py:106
  332.4 13.2 %collective-permute-start.21 = (f32[512,200]{1,0:T(8,128)S(1)}, f32[512,200]{1,0:T(8,128)S(1)}, u32[]{:S(2)}, u32[]{:S(2)}) collective-permute-start(f32[512,200]{1,0:T(8,128)S(1)} %pad_maximum_fusion.15), channel_id=1, source_target_pairs={{0,1},{1,0},{2,3},{3,2},{4,5},{5,4},{6,7},{7,6},{8,9},{9,8},{10,11... | collective-permute-start | bytes 1228808 | tf_op jit(solution)/shard_map/ppermute | solution.py:106
  343.3 13.1 %collective-permute-start.22 = (f32[512,200]{1,0:T(8,128)S(1)}, f32[512,200]{1,0:T(8,128)S(1)}, u32[]{:S(2)}, u32[]{:S(2)}) collective-permute-start(f32[512,200]{1,0:T(8,128)S(1)} %pad_maximum_fusion.15), channel_id=1, source_target_pairs={{0,2},{1,3},{2,0},{3,1},{4,6},{5,7},{6,4},{7,5},{8,10},{9,11},{10,... | collective-permute-start | bytes 1228808 | tf_op jit(solution)/shard_map/ppermute | solution.py:106
  343.8 24.4 %collective-permute-start.23 = (f32[512,200]{1,0:T(8,128)S(1)}, f32[512,200]{1,0:T(8,128)S(1)}, u32[]{:S(2)}, u32[]{:S(2)}) collective-permute-start(f32[512,200]{1,0:T(8,128)S(1)} %pad_maximum_fusion.15), channel_id=1, source_target_pairs={{0,3},{1,2},{2,1},{3,0},{4,7},{5,6},{6,5},{7,4},{8,11},{9,10},{10,... | collective-permute-start | bytes 1228808 | tf_op jit(solution)/shard_map/ppermute | solution.py:106
  414.8 13.2 %collective-permute-start.25 = (f32[512,200]{1,0:T(8,128)S(1)}, f32[512,200]{1,0:T(8,128)S(1)}, u32[]{:S(2)}, u32[]{:S(2)}) collective-permute-start(f32[512,200]{1,0:T(8,128)S(1)} %get-tuple-element.62), channel_id=1, source_target_pairs={{0,2},{1,3},{2,0},{3,1},{4,6},{5,7},{6,4},{7,5},{8,10},{9,11},{10,... | collective-permute-start | bytes 1228808 | tf_op jit(solution)/shard_map/ppermute | solution.py:99
  415.4 24.4 %collective-permute-start.26 = (f32[512,200]{1,0:T(8,128)S(1)}, f32[512,200]{1,0:T(8,128)S(1)}, u32[]{:S(2)}, u32[]{:S(2)}) collective-permute-start(f32[512,200]{1,0:T(8,128)S(1)} %get-tuple-element.63), channel_id=1, source_target_pairs={{0,3},{1,2},{2,1},{3,0},{4,7},{5,6},{6,5},{7,4},{8,11},{9,10},{10,... | collective-permute-start | bytes 1228808 | tf_op jit(solution)/shard_map/ppermute | solution.py:99
  440.0 9.0 %collective-permute-start.27 = (f32[128,200]{1,0:T(8,128)S(1)}, f32[128,200]{1,0:T(8,128)S(1)}, u32[]{:S(2)}, u32[]{:S(2)}) collective-permute-start(f32[128,200]{1,0:T(8,128)S(1)} %get-tuple-element.97), channel_id=1, source_target_pairs={{0,4},{1,5},{2,6},{3,7},{4,0},{5,1},{6,2},{7,3},{8,12},{9,13},{10,... | collective-permute-start | bytes 307208 | tf_op jit(solution)/shard_map/ppermute | solution.py:99
  442.6 6.4 %collective-permute-start.28 = (f32[128,200]{1,0:T(8,128)S(1)}, f32[128,200]{1,0:T(8,128)S(1)}, u32[]{:S(2)}, u32[]{:S(2)}) collective-permute-start(f32[128,200]{1,0:T(8,128)S(1)} %get-tuple-element.99), channel_id=1, source_target_pairs={{0,8},{1,9},{2,10},{3,11},{4,12},{5,13},{6,14},{7,15},{8,0},{9,1},... | collective-permute-start | bytes 307208 | tf_op jit(solution)/shard_map/ppermute | solution.py:99
  443.6 10.5 %collective-permute-start.29 = (f32[128,200]{1,0:T(8,128)S(1)}, f32[128,200]{1,0:T(8,128)S(1)}, u32[]{:S(2)}, u32[]{:S(2)}) collective-permute-start(f32[128,200]{1,0:T(8,128)S(1)} %get-tuple-element.98), channel_id=1, source_target_pairs={{0,12},{1,13},{2,14},{3,15},{4,8},{5,9},{6,10},{7,11},{8,4},{9,5},... | collective-permute-start | bytes 307208 | tf_op jit(solution)/shard_map/ppermute | solution.py:99
  454.2 7.3 %collective-permute-start.30 = (f32[32,200]{1,0:T(8,128)S(1)}, f32[32,200]{1,0:T(8,128)S(1)}, u32[]{:S(2)}, u32[]{:S(2)}) collective-permute-start(f32[32,200]{1,0:T(8,128)S(1)} %get-tuple-element.129), channel_id=1, source_target_pairs={{0,16},{1,17},{2,18},{3,19},{4,20},{5,21},{6,22},{7,23},{8,24},{9,... | collective-permute-start | bytes 76808 | tf_op jit(solution)/shard_map/ppermute | solution.py:99
  459.0 7.9 %collective-permute-start.32 = (f32[32,200]{1,0:T(8,128)S(1)}, f32[32,200]{1,0:T(8,128)S(1)}, u32[]{:S(2)}, u32[]{:S(2)}) collective-permute-start(f32[32,200]{1,0:T(8,128)S(1)} %get-tuple-element.130), channel_id=1, source_target_pairs={{0,48},{1,49},{2,50},{3,51},{4,52},{5,53},{6,54},{7,55},{8,56},{9,... | collective-permute-start | bytes 76808 | tf_op jit(solution)/shard_map/ppermute | solution.py:99
  485.8 7.0 %collective-permute-start.39 = (f32[32,200]{1,0:T(8,128)S(1)}, f32[32,200]{1,0:T(8,128)S(1)}, u32[]{:S(2)}, u32[]{:S(2)}) collective-permute-start(f32[32,200]{1,0:T(8,128)S(1)} %pad_maximum_fusion.21), channel_id=1, source_target_pairs={{0,16},{1,17},{2,18},{3,19},{4,20},{5,21},{6,22},{7,23},{8,24},{9,... | collective-permute-start | bytes 76808 | tf_op jit(solution)/shard_map/ppermute | solution.py:106
  488.2 7.9 %collective-permute-start.41 = (f32[32,200]{1,0:T(8,128)S(1)}, f32[32,200]{1,0:T(8,128)S(1)}, u32[]{:S(2)}, u32[]{:S(2)}) collective-permute-start(f32[32,200]{1,0:T(8,128)S(1)} %pad_maximum_fusion.21), channel_id=1, source_target_pairs={{0,48},{1,49},{2,50},{3,51},{4,52},{5,53},{6,54},{7,55},{8,56},{9,... | collective-permute-start | bytes 76808 | tf_op jit(solution)/shard_map/ppermute | solution.py:106
  498.8 8.0 %collective-permute-start.43 = (f32[128,200]{1,0:T(8,128)S(1)}, f32[128,200]{1,0:T(8,128)S(1)}, u32[]{:S(2)}, u32[]{:S(2)}) collective-permute-start(f32[128,200]{1,0:T(8,128)S(1)} %pad_maximum_fusion.18), channel_id=1, source_target_pairs={{0,8},{1,9},{2,10},{3,11},{4,12},{5,13},{6,14},{7,15},{8,0},{9,1},... | collective-permute-start | bytes 307208 | tf_op jit(solution)/shard_map/ppermute | solution.py:106
  499.8 7.0 %collective-permute-start.44 = (f32[128,200]{1,0:T(8,128)S(1)}, f32[128,200]{1,0:T(8,128)S(1)}, u32[]{:S(2)}, u32[]{:S(2)}) collective-permute-start(f32[128,200]{1,0:T(8,128)S(1)} %pad_maximum_fusion.18), channel_id=1, source_target_pairs={{0,12},{1,13},{2,14},{3,15},{4,8},{5,9},{6,10},{7,11},{8,4},{9,5},... | collective-permute-start | bytes 307208 | tf_op jit(solution)/shard_map/ppermute | solution.py:106
  506.9 12.7 %collective-permute-start.45 = (f32[512,200]{1,0:T(8,128)S(1)}, f32[512,200]{1,0:T(8,128)S(1)}, u32[]{:S(2)}, u32[]{:S(2)}) collective-permute-start(f32[512,200]{1,0:T(8,128)S(1)} %pad_maximum_fusion.16), channel_id=1, source_target_pairs={{0,1},{1,0},{2,3},{3,2},{4,5},{5,4},{6,7},{7,6},{8,9},{9,8},{10,11... | collective-permute-start | bytes 1228808 | tf_op jit(solution)/shard_map/ppermute | solution.py:106
  516.4 13.4 %collective-permute-start.46 = (f32[512,200]{1,0:T(8,128)S(1)}, f32[512,200]{1,0:T(8,128)S(1)}, u32[]{:S(2)}, u32[]{:S(2)}) collective-permute-start(f32[512,200]{1,0:T(8,128)S(1)} %pad_maximum_fusion.16), channel_id=1, source_target_pairs={{0,2},{1,3},{2,0},{3,1},{4,6},{5,7},{6,4},{7,5},{8,10},{9,11},{10,... | collective-permute-start | bytes 1228808 | tf_op jit(solution)/shard_map/ppermute | solution.py:106
  516.7 24.6 %collective-permute-start.47 = (f32[512,200]{1,0:T(8,128)S(1)}, f32[512,200]{1,0:T(8,128)S(1)}, u32[]{:S(2)}, u32[]{:S(2)}) collective-permute-start(f32[512,200]{1,0:T(8,128)S(1)} %pad_maximum_fusion.16), channel_id=1, source_target_pairs={{0,3},{1,2},{2,1},{3,0},{4,7},{5,6},{6,5},{7,4},{8,11},{9,10},{10,... | collective-permute-start | bytes 1228808 | tf_op jit(solution)/shard_map/ppermute | solution.py:106
  (61 other events, 733.6 us)
Sparse Core Ops, SparseCore 0:
  12.2 139.2 all-gather.2
  226.3 123.0 all-gather.4

commit v3 on v1

--- a/solution.py
+++ b/solution.py
@@ -75,6 +75,54 @@
         strip_parts(gathered[:, :depth], neighbours, fold_flag),
         strip_parts(gathered[:, depth:], neighbours, fold_flag),
     )
+
+
+def exchange_rims(fields, neighbours, fold_flag):
+    amount = lax.psum(1, "space")
+    own = neighbours[0]
+    dest = jnp.arange(amount, dtype=own.dtype)
+
+    def toward(directions):
+        hit = jnp.zeros((amount,), jnp.bool_)
+        for k in directions:
+            hit = hit | (own[k] == dest)
+        return hit[:, None, None]
+
+    up, down = toward((0, 4, 5)), toward((1, 6, 7))
+    east, west = toward((2,)), toward((3,))
+    slots = []
+    for field in fields:
+        extent = field.shape[2]
+        row_low, row_high = field[0, :, 0, :], field[0, :, extent - 1, :]
+        col_low, col_high = field[0, :, :, 0], field[0, :, :, extent - 1]
+        empty = jnp.zeros_like(row_low)[None]
+        slots.append(jnp.where(up, row_high[None], jnp.where(down, row_low[None], empty)))
+        slots.append(jnp.where(east, col_high[None], jnp.where(west, col_low[None], empty)))
+    got = lax.all_to_all(jnp.concatenate(slots, axis=2), "space", 0, 0, tiled=True)
+    found = []
+    for n, field in enumerate(fields):
+        extent = field.shape[2]
+        rows = got[:, :, 2 * n * extent : (2 * n + 1) * extent]
+        cols = got[:, :, (2 * n + 1) * extent : (2 * n + 2) * extent]
+
+        def pick(part, k):
+            index = neighbours[:, k]
+            valid = ((index >= 0) & (index < amount)).astype(part.dtype)
+            return jnp.take(part, jnp.clip(index, 0, amount - 1), axis=0) * valid[:, None, None]
+
+        from_north = pick(rows, 0)
+        north = jnp.where((fold_flag == 1)[:, None, None], from_north[:, :, ::-1], from_north)
+        corners = jnp.stack(
+            [
+                pick(rows, 4)[:, :, 0],
+                pick(rows, 5)[:, :, extent - 1],
+                pick(rows, 6)[:, :, 0],
+                pick(rows, 7)[:, :, extent - 1],
+            ],
+            axis=-1,
+        )
+        found.append((north, pick(rows, 1), pick(cols, 2), pick(cols, 3), corners))
+    return found
 
 
 REDUCE_AXES = ("space", "dp")
@@ -168,15 +216,13 @@
     water_indicator = ocean.astype(jnp.float32)[:, None, :]
     masked_grad = (loss_sensitivity[0].astype(jnp.float32) * water_indicator).astype(jnp.bfloat16)
     grad_tiles = masked_grad.reshape(patch_total, feature_depth, patch_extent, patch_extent)
-    field_parts, grad_parts = collect_two_rims(
-        edge_strips(inputs), edge_strips(grad_tiles), neighbours, fold_flag
-    )
+    field_parts, grad_parts = exchange_rims((inputs, grad_tiles), neighbours, fold_flag)
     in_padded = padded_tiles(inputs, field_parts)
     pre_first = conv_forward(in_padded, w_first)
     value, slope = gelu_pair(pre_first)
     hidden = (value * water_indicator).astype(jnp.bfloat16)
     hidden_tiles = hidden.reshape(patch_total, feature_depth, patch_extent, patch_extent)
-    hidden_parts = collect_rims(edge_strips(hidden_tiles), neighbours, fold_flag)
+    (hidden_parts,) = exchange_rims((hidden_tiles,), neighbours, fold_flag)
     hidden_padded = padded_tiles(hidden_tiles, hidden_parts)
     latter_linear_response = conv_forward(hidden_padded, w_second)
     prediction = (latter_linear_response * water_indicator).astype(jnp.bfloat16)[None]

time: 496 us -> 430 us (0.87)
  waiting for transfers between devices: 267 us -> 170 us
  starting transfers between devices: 65.3 us -> 105 us
  between operations: 31.1 us -> 18.2 us
  other arithmetic: 23 us -> 33.9 us
  local copies, waits for them, and re-layouts: 61.4 us -> 54.3 us
    all_gather x2 -> x0, waiting for transfers between devices: 183 us -> none  [the longest x1 124 us: collect_two_rims(): lax.all_gather(jnp.concatenate([first, second], axis=1), 'space', axis=0,...]
    all_to_all x0 -> x2, waiting for transfers between devices: none -> 57.7 us  [exchange_rims(): lax.all_to_all(jnp.concatenate(slots, axis=2), 'space', 0, 0, tiled=True)]
    ppermute x16, waiting for transfers between devices: 45.9 us -> 74.9 us  [all_sum(): buf = keep + lax.ppermute(send, REDUCE_AXES, pairs)]
    all_to_all x0 -> x2, starting transfers between devices: none -> 22.1 us  [exchange_rims(): lax.all_to_all(jnp.concatenate(slots, axis=2), 'space', 0, 0, tiled=True)]
    ppermute x16, starting transfers between devices: 30.1 us -> 46.3 us  [all_sum(): buf = keep + lax.ppermute(send, REDUCE_AXES, pairs)]
    slice x26 -> x10, local copies, waits for them, and re-layouts: 12.4 us -> 6 us  [the longest x1 4.65 us: exchange_rims(): cols = got[:, :, (2 * n + 1) * extent:(2 * n + 2) * extent]]
    unnamed x116 -> x160, local copies, waits for them, and re-layouts: 12.8 us -> 10.3 us
  transfers between devices with their start and end apart: 34 -> 34, of which waited for: 29 -> 26; matrix products, arithmetic and copies ran while one was open for 8% -> 10% of each run, Pallas kernels for 0% -> 0%
where the time goes in v3:
time: 430 us; the launch traced here: 422 us
  waiting for transfers between devices  170 us (40%)
  starting transfers between devices  105 us (24%)
  local copies, waits for them, and re-layouts  54.3 us (13%)
  matrix products  40.3 us (9%)
  other arithmetic  33.9 us (8%)
  between operations  18.2 us (4%)
    ppermute x16, waiting for transfers between devices, all_sum(): buf = keep + lax.ppermute(send, REDUCE_AXES, pairs)  74.9 us
    all_to_all x2, waiting for transfers between devices, exchange_rims(): lax.all_to_all(jnp.concatenate(slots, axis=2), 'space', 0, 0, tiled=True)  57.7 us
    ppermute x16, starting transfers between devices, all_sum(): buf = keep + lax.ppermute(send, REDUCE_AXES, pairs)  46.3 us
    ppermute x16, waiting for transfers between devices, all_sum(): recv = lax.ppermute(buf, REDUCE_AXES, pairs)  37.4 us
    ppermute x16, starting transfers between devices, all_sum(): recv = lax.ppermute(buf, REDUCE_AXES, pairs)  36.5 us
    all_to_all x2, starting transfers between devices, exchange_rims(): lax.all_to_all(jnp.concatenate(slots, axis=2), 'space', 0, 0, tiled=True)  22.1 us
    dot_general x18, matrix products, weight_grad(): jnp.einsum('toc,tic->oi', grads, window(padded, k // 3 - 1, k % 3 - 1), p...  19.4 us
    dot_general x18, matrix products, conv_forward(): jnp.einsum('oi,tic->toc', weights[k], window(padded, k // 3 - 1, k % 3 -...  13.9 us
  transfers between devices with their start and end apart: 34, of which 26 were waited for; matrix products, arithmetic and copies ran while one was open for 10% of the time, Pallas kernels for 0%

profile of v3, /device:TPU:1, one launch (start us, length us, event | category | flops | bytes accessed | tf_op | source)
XLA Modules:
  0.0 421.5 jit_solution(15111996185218060806)
XLA Ops:
  12.9 6.0 %copy.77 = bf16[64,200,128]{2,1,0:T(8,128)(2,1)} copy(bf16[64,200,128]{1,2,0:T(8,128)(2,1)} %pad_maximum_fusion) | data formatting | bytes 6553600 | tf_op jit(solution)/shard_map/concatenate | solution.py:101
  18.9 15.2 %all-to-all-start = ((bf16[64,200,128]{2,1,0:T(8,128)(2,1)}), bf16[64,200,128]{2,1,0:T(8,128)(2,1)S(1)}, u32[]{:S(2)}, u32[]{:S(2)}) async-start(bf16[64,200,128]{2,1,0:T(8,128)(2,1)} %copy.77), calls=%async_computation | async-start | bytes 6553600 | tf_op jit(solution)/shard_map/all_to_all | solution.py:101
  49.8 57.7 %all-to-all-done = bf16[64,200,128]{2,1,0:T(8,128)(2,1)S(1)} async-done(((bf16[64,200,128]{2,1,0:T(8,128)(2,1)}), bf16[64,200,128]{2,1,0:T(8,128)(2,1)S(1)}, u32[]{:S(2)}, u32[]{:S(2)}) %all-to-all-start) | async-done | bytes 3276832 | tf_op jit(solution)/shard_map/all_to_all | solution.py:101
  107.5 4.7 %fusion.161 = (bf16[64,200,32]{2,1,0:T(8,128)(2,1)S(1)}, bf16[64,200,32]{2,1,0:T(8,128)(2,1)S(1)}, bf16[64,200,32]{2,1,0:T(8,128)(2,1)}, bf16[64,200,32]{2,1,0:T(8,128)(2,1)}) fusion(bf16[64,200,128]{2,1,0:T(8,128)(2,1)S(1)} %all-to-all-done), kind=kLoop, calls=%fused_computation.357 | loop fusion | bytes 6553600 | tf_op jit(solution)/shard_map/slice | solution.py:106
  144.8 2.6 fusion.34
  156.1 3.4 reshape.753
  160.7 4.9 %collective-permute-start = (f32[180096]{0:T(1024)}, f32[180096]{0:T(1024)}, u32[]{:S(2)}, u32[]{:S(2)}) collective-permute-start(f32[180096]{0:T(1024)} %pad_dynamic-slice_fusion.2), channel_id=1, source_target_pairs={{0,1},{1,0},{2,3},{3,2},{4,5},{5,4},{6,7},{7,6},{8,9},{9,8},{10,11... | collective-permute-start | bytes 2161160 | tf_op jit(solution)/shard_map/ppermute | solution.py:145
  170.1 9.0 %collective-permute-done.1 = f32[90048]{0:T(1024)S(1)} collective-permute-done((f32[90048]{0:T(1024)S(1)}, f32[90048]{0:T(1024)S(1)}, u32[]{:S(2)}, u32[]{:S(2)}) %collective-permute-start.1) | collective-permute-done | bytes 360224 | tf_op jit(solution)/shard_map/ppermute | solution.py:145
  180.8 3.6 collective-permute-done.2
  189.5 6.8 %all-to-all-start.1 = ((bf16[64,200,64]{1,2,0:T(8,128)(2,1)}), bf16[64,200,64]{1,2,0:T(8,128)(2,1)S(1)}, u32[]{:S(2)}, u32[]{:S(2)}) async-start(bf16[64,200,64]{1,2,0:T(8,128)(2,1)} %pad_maximum_fusion.1), calls=%async_computation.1 | async-start | bytes 4194304 | tf_op jit(solution)/shard_map/all_to_all | solution.py:101
  198.8 4.9 %collective-permute-start.4 = (f32[11256]{0:T(1024)}, f32[11256]{0:T(1024)}, u32[]{:S(2)}, u32[]{:S(2)}) collective-permute-start(f32[11256]{0:T(1024)} %dynamic_slice.105), channel_id=1, source_target_pairs={{0,16},{1,17},{2,18},{3,19},{4,20},{5,21},{6,22},{7,23},{8,24},{9,... | collective-permute-start | bytes 135080 | tf_op jit(solution)/shard_map/ppermute | solution.py:145
  203.7 41.5 %collective-permute-done.4 = f32[11256]{0:T(1024)} collective-permute-done((f32[11256]{0:T(1024)}, f32[11256]{0:T(1024)}, u32[]{:S(2)}, u32[]{:S(2)}) %collective-permute-start.4) | collective-permute-done | bytes 45056 | tf_op jit(solution)/shard_map/ppermute | solution.py:145
  280.4 7.1 %collective-permute-done.11 = f32[11256]{0:T(1024)} collective-permute-done((f32[11256]{0:T(1024)}, f32[11256]{0:T(1024)}, u32[]{:S(2)}, u32[]{:S(2)}) %collective-permute-start.11) | collective-permute-done | bytes 45056 | tf_op jit(solution)/shard_map/ppermute | solution.py:149
  303.3 3.4 reshape.755
  307.0 11.9 %collective-permute-start.16 = (f32[180096]{0:T(1024)S(1)}, f32[180096]{0:T(1024)S(1)}, u32[]{:S(2)}, u32[]{:S(2)}) collective-permute-start(f32[180096]{0:T(1024)S(1)} %pad_dynamic-slice_fusion), channel_id=1, source_target_pairs={{0,1},{1,0},{2,3},{3,2},{4,5},{5,4},{6,7},{7,6},{8,9},{9,8},{10,11... | collective-permute-start | bytes 2161160 | tf_op jit(solution)/shard_map/ppermute | solution.py:145
  321.6 4.2 collective-permute-done.13
  325.9 4.8 %collective-permute-done.17 = f32[90048]{0:T(1024)S(1)} collective-permute-done((f32[90048]{0:T(1024)S(1)}, f32[90048]{0:T(1024)S(1)}, u32[]{:S(2)}, u32[]{:S(2)}) %collective-permute-start.17) | collective-permute-done | bytes 360224 | tf_op jit(solution)/shard_map/ppermute | solution.py:145
  332.4 3.1 collective-permute-done.18
  335.7 2.8 collective-permute-start.19
  341.6 3.4 collective-permute-start.20
  345.2 3.9 collective-permute-start.15
  352.4 3.6 collective-permute-start.22
  357.2 3.1 collective-permute-start.23
  361.4 3.0 collective-permute-start.24
  365.8 2.8 collective-permute-start.25
  368.8 3.9 reshape.754
  378.5 4.1 collective-permute-done.27
  384.7 3.3 collective-permute-done.28
  388.6 4.3 %collective-permute-done.29 = f32[45024]{0:T(1024)S(1)} collective-permute-done((f32[45024]{0:T(1024)S(1)}, f32[45024]{0:T(1024)S(1)}, u32[]{:S(2)}, u32[]{:S(2)}) %collective-permute-start.29) | collective-permute-done | bytes 180128 | tf_op jit(solution)/shard_map/ppermute | solution.py:149
  394.1 5.7 %collective-permute-done.30 = f32[90048]{0:T(1024)S(1)} collective-permute-done((f32[90048]{0:T(1024)S(1)}, f32[90048]{0:T(1024)S(1)}, u32[]{:S(2)}, u32[]{:S(2)}) %collective-permute-start.30) | collective-permute-done | bytes 360224 | tf_op jit(solution)/shard_map/ppermute | solution.py:149
  400.1 14.9 %collective-permute-start.31 = (f32[180096]{0:T(1024)S(1)}, f32[180096]{0:T(1024)S(1)}, u32[]{:S(2)}, u32[]{:S(2)}) collective-permute-start(f32[180096]{0:T(1024)S(1)} %pad_maximum_fusion.5), channel_id=1, source_target_pairs={{0,1},{1,0},{2,3},{3,2},{4,5},{5,4},{6,7},{7,6},{8,9},{9,8},{10,11... | collective-permute-start | bytes 2161160 | tf_op jit(solution)/shard_map/ppermute | solution.py:149
  417.1 3.9 reshape.756
  (392 shorter events, 145.8 us)
Async XLA Ops:
  18.9 88.6 %all-to-all-start = ((bf16[64,200,128]{2,1,0:T(8,128)(2,1)}), bf16[64,200,128]{2,1,0:T(8,128)(2,1)S(1)}, u32[]{:S(2)}, u32[]{:S(2)}) async-start(bf16[64,200,128]{2,1,0:T(8,128)(2,1)} %copy.77), calls=%async_computation | async-start | bytes 6553600 | tf_op jit(solution)/shard_map/all_to_all | solution.py:101
  160.7 7.0 %collective-permute-start = (f32[180096]{0:T(1024)}, f32[180096]{0:T(1024)}, u32[]{:S(2)}, u32[]{:S(2)}) collective-permute-start(f32[180096]{0:T(1024)} %pad_dynamic-slice_fusion.2), channel_id=1, source_target_pairs={{0,1},{1,0},{2,3},{3,2},{4,5},{5,4},{6,7},{7,6},{8,9},{9,8},{10,11... | collective-permute-start | bytes 2161160 | tf_op jit(solution)/shard_map/ppermute | solution.py:145
  169.3 9.9 %collective-permute-start.1 = (f32[90048]{0:T(1024)S(1)}, f32[90048]{0:T(1024)S(1)}, u32[]{:S(2)}, u32[]{:S(2)}) collective-permute-start(f32[90048]{0:T(1024)S(1)} %dynamic_slice.99), channel_id=1, source_target_pairs={{0,2},{1,3},{2,0},{3,1},{4,6},{5,7},{6,4},{7,5},{8,10},{9,11},{10,... | collective-permute-start | bytes 1080584 | tf_op jit(solution)/shard_map/ppermute | solution.py:145
  179.4 5.0 %collective-permute-start.2 = (f32[45024]{0:T(1024)S(1)}, f32[45024]{0:T(1024)S(1)}, u32[]{:S(2)}, u32[]{:S(2)}) collective-permute-start(f32[45024]{0:T(1024)S(1)} %dynamic_slice.101), channel_id=1, source_target_pairs={{0,4},{1,5},{2,6},{3,7},{4,0},{5,1},{6,2},{7,3},{8,12},{9,13},{10,... | collective-permute-start | bytes 540296 | tf_op jit(solution)/shard_map/ppermute | solution.py:145
  185.9 10.4 %collective-permute-start.3 = (f32[22512]{0:T(1024)}, f32[22512]{0:T(1024)}, u32[]{:S(2)}, u32[]{:S(2)}) collective-permute-start(f32[22512]{0:T(1024)} %dynamic_slice.103), channel_id=1, source_target_pairs={{0,8},{1,9},{2,10},{3,11},{4,12},{5,13},{6,14},{7,15},{8,0},{9,1},... | collective-permute-start | bytes 270152 | tf_op jit(solution)/shard_map/ppermute | solution.py:145
  189.5 100.1 %all-to-all-start.1 = ((bf16[64,200,64]{1,2,0:T(8,128)(2,1)}), bf16[64,200,64]{1,2,0:T(8,128)(2,1)S(1)}, u32[]{:S(2)}, u32[]{:S(2)}) async-start(bf16[64,200,64]{1,2,0:T(8,128)(2,1)} %pad_maximum_fusion.1), calls=%async_computation.1 | async-start | bytes 4194304 | tf_op jit(solution)/shard_map/all_to_all | solution.py:101
  198.8 46.4 %collective-permute-start.4 = (f32[11256]{0:T(1024)}, f32[11256]{0:T(1024)}, u32[]{:S(2)}, u32[]{:S(2)}) collective-permute-start(f32[11256]{0:T(1024)} %dynamic_slice.105), channel_id=1, source_target_pairs={{0,16},{1,17},{2,18},{3,19},{4,20},{5,21},{6,22},{7,23},{8,24},{9,... | collective-permute-start | bytes 135080 | tf_op jit(solution)/shard_map/ppermute | solution.py:145
  247.4 3.0 collective-permute-start.5
  251.9 4.2 collective-permute-start.6
  257.6 4.5 %collective-permute-start.7 = (f32[1407]{0:T(1024)}, f32[1407]{0:T(1024)}, u32[]{:S(2)}, u32[]{:S(2)}) collective-permute-start(f32[1407]{0:T(1024)} %dynamic_slice.111), channel_id=1, source_target_pairs={{0,128},{1,129},{2,130},{3,131},{4,132},{5,133},{6,134},{7,135},{8... | collective-permute-start | bytes 16892 | tf_op jit(solution)/shard_map/ppermute | solution.py:145
  263.5 4.2 %collective-permute-start.8 = (f32[1407]{0:T(1024)}, f32[1407]{0:T(1024)S(1)}, u32[]{:S(2)}, u32[]{:S(2)}) collective-permute-start(f32[1407]{0:T(1024)} %dynamic-slice_add_fusion.13), channel_id=1, source_target_pairs={{0,128},{1,129},{2,130},{3,131},{4,132},{5,133},{6,134},{7,135},{8... | collective-permute-start | bytes 16892 | tf_op jit(solution)/shard_map/ppermute | solution.py:149
  269.0 4.2 collective-permute-start.9
  280.4 7.1 %collective-permute-start.11 = (f32[11256]{0:T(1024)}, f32[11256]{0:T(1024)}, u32[]{:S(2)}, u32[]{:S(2)}) collective-permute-start(f32[11256]{0:T(1024)} %pad_maximum_fusion.21), channel_id=1, source_target_pairs={{0,16},{1,17},{2,18},{3,19},{4,20},{5,21},{6,22},{7,23},{8,24},{9,... | collective-permute-start | bytes 135080 | tf_op jit(solution)/shard_map/ppermute | solution.py:149
  289.2 29.8 %collective-permute-start.12 = (f32[22512]{0:T(1024)}, f32[22512]{0:T(1024)}, u32[]{:S(2)}, u32[]{:S(2)}) collective-permute-start(f32[22512]{0:T(1024)} %pad_maximum_fusion.19), channel_id=1, source_target_pairs={{0,8},{1,9},{2,10},{3,11},{4,12},{5,13},{6,14},{7,15},{8,0},{9,1},... | collective-permute-start | bytes 270152 | tf_op jit(solution)/shard_map/ppermute | solution.py:149
  307.0 13.8 %collective-permute-start.16 = (f32[180096]{0:T(1024)S(1)}, f32[180096]{0:T(1024)S(1)}, u32[]{:S(2)}, u32[]{:S(2)}) collective-permute-start(f32[180096]{0:T(1024)S(1)} %pad_dynamic-slice_fusion), channel_id=1, source_target_pairs={{0,1},{1,0},{2,3},{3,2},{4,5},{5,4},{6,7},{7,6},{8,9},{9,8},{10,11... | collective-permute-start | bytes 2161160 | tf_op jit(solution)/shard_map/ppermute | solution.py:145
  320.0 5.8 %collective-permute-start.13 = (f32[45024]{0:T(1024)S(1)}, f32[45024]{0:T(1024)S(1)}, u32[]{:S(2)}, u32[]{:S(2)}) collective-permute-start(f32[45024]{0:T(1024)S(1)} %pad_maximum_fusion.17), channel_id=1, source_target_pairs={{0,4},{1,5},{2,6},{3,7},{4,0},{5,1},{6,2},{7,3},{8,12},{9,13},{10,... | collective-permute-start | bytes 540296 | tf_op jit(solution)/shard_map/ppermute | solution.py:149
  321.3 9.4 %collective-permute-start.17 = (f32[90048]{0:T(1024)S(1)}, f32[90048]{0:T(1024)S(1)}, u32[]{:S(2)}, u32[]{:S(2)}) collective-permute-start(f32[90048]{0:T(1024)S(1)} %dynamic_slice.115), channel_id=1, source_target_pairs={{0,2},{1,3},{2,0},{3,1},{4,6},{5,7},{6,4},{7,5},{8,10},{9,11},{10,... | collective-permute-start | bytes 1080584 | tf_op jit(solution)/shard_map/ppermute | solution.py:145
  331.0 4.4 %collective-permute-start.18 = (f32[45024]{0:T(1024)S(1)}, f32[45024]{0:T(1024)S(1)}, u32[]{:S(2)}, u32[]{:S(2)}) collective-permute-start(f32[45024]{0:T(1024)S(1)} %dynamic_slice.117), channel_id=1, source_target_pairs={{0,4},{1,5},{2,6},{3,7},{4,0},{5,1},{6,2},{7,3},{8,12},{9,13},{10,... | collective-permute-start | bytes 540296 | tf_op jit(solution)/shard_map/ppermute | solution.py:145
  332.0 8.2 %collective-permute-start.14 = (f32[90048]{0:T(1024)S(1)}, f32[90048]{0:T(1024)S(1)}, u32[]{:S(2)}, u32[]{:S(2)}) collective-permute-start(f32[90048]{0:T(1024)S(1)} %pad_maximum_fusion.15), channel_id=1, source_target_pairs={{0,2},{1,3},{2,0},{3,1},{4,6},{5,7},{6,4},{7,5},{8,10},{9,11},{10,... | collective-permute-start | bytes 1080584 | tf_op jit(solution)/shard_map/ppermute | solution.py:149
  335.7 5.7 %collective-permute-start.19 = (f32[22512]{0:T(1024)S(1)}, f32[22512]{0:T(1024)S(1)}, u32[]{:S(2)}, u32[]{:S(2)}) collective-permute-start(f32[22512]{0:T(1024)S(1)} %dynamic_slice.119), channel_id=1, source_target_pairs={{0,8},{1,9},{2,10},{3,11},{4,12},{5,13},{6,14},{7,15},{8,0},{9,1},... | collective-permute-start | bytes 270152 | tf_op jit(solution)/shard_map/ppermute | solution.py:145
  341.6 7.5 %collective-permute-start.20 = (f32[11256]{0:T(1024)S(1)}, f32[11256]{0:T(1024)S(1)}, u32[]{:S(2)}, u32[]{:S(2)}) collective-permute-start(f32[11256]{0:T(1024)S(1)} %dynamic_slice.121), channel_id=1, source_target_pairs={{0,16},{1,17},{2,18},{3,19},{4,20},{5,21},{6,22},{7,23},{8,24},{9,... | collective-permute-start | bytes 135080 | tf_op jit(solution)/shard_map/ppermute | solution.py:145
  345.2 19.3 %collective-permute-start.15 = (f32[180096]{0:T(1024)S(1)}, f32[180096]{0:T(1024)}, u32[]{:S(2)}, u32[]{:S(2)}) collective-permute-start(f32[180096]{0:T(1024)S(1)} %pad_maximum_fusion.4), channel_id=1, source_target_pairs={{0,1},{1,0},{2,3},{3,2},{4,5},{5,4},{6,7},{7,6},{8,9},{9,8},{10,11... | collective-permute-start | bytes 2161160 | tf_op jit(solution)/shard_map/ppermute | solution.py:149
  349.3 3.0 collective-permute-start.21
  352.4 4.7 %collective-permute-start.22 = (f32[2814]{0:T(1024)S(1)}, f32[2814]{0:T(1024)S(1)}, u32[]{:S(2)}, u32[]{:S(2)}) collective-permute-start(f32[2814]{0:T(1024)S(1)} %dynamic_slice.125), channel_id=1, source_target_pairs={{0,64},{1,65},{2,66},{3,67},{4,68},{5,69},{6,70},{7,71},{8,72},{9,... | collective-permute-start | bytes 33776 | tf_op jit(solution)/shard_map/ppermute | solution.py:145
  357.2 4.1 collective-permute-start.23
  361.4 4.3 %collective-permute-start.24 = (f32[1407]{0:T(1024)S(1)}, f32[1407]{0:T(1024)S(1)}, u32[]{:S(2)}, u32[]{:S(2)}) collective-permute-start(f32[1407]{0:T(1024)S(1)} %dynamic-slice_add_fusion.12), channel_id=1, source_target_pairs={{0,128},{1,129},{2,130},{3,131},{4,132},{5,133},{6,134},{7,135},{8... | collective-permute-start | bytes 16892 | tf_op jit(solution)/shard_map/ppermute | solution.py:149
  365.8 6.8 %collective-permute-start.25 = (f32[2814]{0:T(1024)S(1)}, f32[2814]{0:T(1024)S(1)}, u32[]{:S(2)}, u32[]{:S(2)}) collective-permute-start(f32[2814]{0:T(1024)S(1)} %pad_maximum_fusion.28), channel_id=1, source_target_pairs={{0,64},{1,65},{2,66},{3,67},{4,68},{5,69},{6,70},{7,71},{8,72},{9,... | collective-permute-start | bytes 33776 | tf_op jit(solution)/shard_map/ppermute | solution.py:149
  375.7 6.8 %collective-permute-start.27 = (f32[11256]{0:T(1024)S(1)}, f32[11256]{0:T(1024)S(1)}, u32[]{:S(2)}, u32[]{:S(2)}) collective-permute-start(f32[11256]{0:T(1024)S(1)} %pad_maximum_fusion.22), channel_id=1, source_target_pairs={{0,16},{1,17},{2,18},{3,19},{4,20},{5,21},{6,22},{7,23},{8,24},{9,... | collective-permute-start | bytes 135080 | tf_op jit(solution)/shard_map/ppermute | solution.py:149
  382.7 5.3 %collective-permute-start.28 = (f32[22512]{0:T(1024)S(1)}, f32[22512]{0:T(1024)S(1)}, u32[]{:S(2)}, u32[]{:S(2)}) collective-permute-start(f32[22512]{0:T(1024)S(1)} %pad_maximum_fusion.20), channel_id=1, source_target_pairs={{0,8},{1,9},{2,10},{3,11},{4,12},{5,13},{6,14},{7,15},{8,0},{9,1},... | collective-permute-start | bytes 270152 | tf_op jit(solution)/shard_map/ppermute | solution.py:149
  388.2 4.7 %collective-permute-start.29 = (f32[45024]{0:T(1024)S(1)}, f32[45024]{0:T(1024)S(1)}, u32[]{:S(2)}, u32[]{:S(2)}) collective-permute-start(f32[45024]{0:T(1024)S(1)} %pad_maximum_fusion.18), channel_id=1, source_target_pairs={{0,4},{1,5},{2,6},{3,7},{4,0},{5,1},{6,2},{7,3},{8,12},{9,13},{10,... | collective-permute-start | bytes 540296 | tf_op jit(solution)/shard_map/ppermute | solution.py:149
  393.1 6.7 %collective-permute-start.30 = (f32[90048]{0:T(1024)S(1)}, f32[90048]{0:T(1024)S(1)}, u32[]{:S(2)}, u32[]{:S(2)}) collective-permute-start(f32[90048]{0:T(1024)S(1)} %pad_maximum_fusion.16), channel_id=1, source_target_pairs={{0,2},{1,3},{2,0},{3,1},{4,6},{5,7},{6,4},{7,5},{8,10},{9,11},{10,... | collective-permute-start | bytes 1080584 | tf_op jit(solution)/shard_map/ppermute | solution.py:149
  400.1 16.8 %collective-permute-start.31 = (f32[180096]{0:T(1024)S(1)}, f32[180096]{0:T(1024)S(1)}, u32[]{:S(2)}, u32[]{:S(2)}) collective-permute-start(f32[180096]{0:T(1024)S(1)} %pad_maximum_fusion.5), channel_id=1, source_target_pairs={{0,1},{1,0},{2,3},{3,2},{4,5},{5,4},{6,7},{7,6},{8,9},{9,8},{10,11... | collective-permute-start | bytes 2161160 | tf_op jit(solution)/shard_map/ppermute | solution.py:149
  (70 other events, 392.2 us)
